TPU v7x, 128 devices: a whole 4x4x4 slice. The times are simulated.
128 devices in a mesh: seq: 16 (over x, y), head: 8 (over z, core).
Axes of the slice: x: 4, y: 4, z: 4, core: 2. Of those that a mesh axis runs over, the one named last changes fastest.
Arguments:
- ssd_input: bfloat16 [4096, 8192], P('seq', 'head'), may hold values from -6 to 6
- gate_input: bfloat16 [4096, 8192], P('seq', 'head'), may hold values from -6 to 6
- write_vectors: bfloat16 [4096, 2048], P('seq', 'head'), may hold values from -1 to 1
- read_vectors: bfloat16 [4096, 2048], P('seq', 'head'), may hold values from -6 to 6
- log_decay: float32 [4096, 128], P('seq', 'head'), may hold values from -1 to 0
- skip_gain: float32 [128], P('head'), may hold values from 0.5 to 1.5
- norm_gain: float32 [8192], P('head'), may hold values from 0.5 to 1.5
- out_weight: bfloat16 [8192, 8192], P(None, 'head'), may hold values from -0.0625 to 0.0625
- out_grad: bfloat16 [4096, 8192], P('seq', 'head'), may hold values from -6 to 6
Outputs:
- layer_out: bfloat16 [4096, 8192], P('seq', 'head')
- input_grad: bfloat16 [4096, 8192], P('seq', 'head')
- gate_grad: bfloat16 [4096, 8192], P('seq', 'head')
- write_grad: bfloat16 [4096, 2048], P('seq', 'head')
- read_grad: bfloat16 [4096, 2048], P('seq', 'head')
- decay_grad: float32 [4096, 128], P('seq', 'head')
- weight_grad: bfloat16 [8192, 8192], P('seq', 'head')
All inputs are finite; a program needn't handle non-finite values.
Results may differ from a plain program's by a relative error of at most 0.018.
Values may be sent and summed in bfloat16 or wider, within the bound.
No kernel may reach another device: no remote copies, remote signals or barrier semaphores. Data moves between devices by JAX's collectives and lax.ppermute only.
A program may use at most 192 MiB of HBM per device.

v0:
```python
from functools import partial

import jax
import jax.numpy as jnp
from jax import lax
from jax.sharding import PartitionSpec as P

HALF_HEADS = 128
P_SIZE = 64
N = 256
G = 8
SPAN = 256


epsilon = 1e-05
highest = lax.Precision.HIGHEST


def entering(x, axis, join, neutral):
    place = lax.axis_index(axis)
    gathered = jax.tree.map(
        lambda a, kind: lax.all_gather(a.astype(kind), axis), x, (jnp.bfloat16, jnp.bfloat16)
    )
    state = jax.tree.map(lambda a, e: jnp.zeros_like(a) + jnp.asarray(e, a.dtype), x, neutral)

    def entering_one(hop, state):
        return join(
            state,
            jax.tree.map(
                lambda a, own: lax.dynamic_index_in_dim(a, hop, 0, False).astype(own.dtype),
                gathered,
                x,
            ),
        )

    return lax.fori_loop(0, place, entering_one, state)


def prefix(x, axis, join, neutral):
    count = lax.axis_size(axis)
    place = lax.axis_index(axis)
    ahead = count - 1 - place
    gathered = jax.tree.map(
        lambda a, kind: lax.all_gather(a.astype(kind), axis),
        x,
        jax.tree.map(lambda a: jnp.bfloat16 if a.dtype == jnp.float32 else a.dtype, x),
    )
    state = jax.tree.map(lambda a, e: jnp.zeros_like(a) + jnp.asarray(e, a.dtype), x, neutral)

    def prefix_one(hop, state):
        source = count - 1 - hop
        return join(
            state,
            jax.tree.map(
                lambda a, own: lax.dynamic_index_in_dim(a, source, 0, False).astype(own.dtype),
                gathered,
                x,
            ),
        )

    return lax.fori_loop(0, ahead, prefix_one, state)


def block_scan(state_now, pieces):
    input_block, write_block, read_block, decay_block = pieces
    row_count = decay_block.shape[0]
    group_count, per_group = (state_now.shape[0], state_now.shape[1])
    input_heads = input_block.reshape(row_count, group_count, per_group, P_SIZE)
    write_heads = write_block.reshape(row_count, group_count, N)
    read_heads = read_block.reshape(row_count, group_count, N)
    cumulative = jnp.cumsum(decay_block, axis=0).reshape(row_count, group_count, per_group)
    by_head = jnp.transpose(cumulative, (1, 2, 0))
    causal = lax.broadcasted_iota(jnp.int32, (row_count, row_count), 0) >= lax.broadcasted_iota(
        jnp.int32, (row_count, row_count), 1
    )
    gap_table = jnp.where(causal, by_head[..., :, None] - by_head[..., None, :], 0.0)
    decay_table = jnp.where(causal, jnp.exp(gap_table), 0.0)
    scores = jnp.einsum("tgn,sgn->gts", read_heads, write_heads, precision=highest)
    weights = scores[:, None] * decay_table
    inner_sum = jnp.einsum("gkts,sgkp->tgkp", weights, input_heads, precision=highest)
    carried = jnp.einsum("tgn,gkpn->tgkp", read_heads, state_now, precision=highest)
    output = inner_sum + jnp.exp(cumulative)[..., None] * carried
    final_log = cumulative[-1]
    weighted = input_heads * jnp.exp(final_log[None] - cumulative)[..., None]
    fresh_state = jnp.einsum("sgkp,sgn->gkpn", weighted, write_heads, precision=highest)
    next_state = jnp.exp(final_log)[..., None, None] * state_now + fresh_state
    return (next_state, output.reshape(row_count, group_count * per_group * P_SIZE))


def block_end(state_now, pieces):
    input_block, write_block, decay_block = pieces
    row_count = decay_block.shape[0]
    group_count, per_group = (state_now.shape[0], state_now.shape[1])
    input_heads = input_block.reshape(row_count, group_count, per_group, P_SIZE)
    write_heads = write_block.reshape(row_count, group_count, N)
    cumulative = jnp.cumsum(decay_block, axis=0).reshape(row_count, group_count, per_group)
    final_log = cumulative[-1]
    weighted = input_heads * jnp.exp(final_log[None] - cumulative)[..., None]
    fresh_state = jnp.einsum("sgkp,sgn->gkpn", weighted, write_heads, precision=highest)
    return (jnp.exp(final_log)[..., None, None] * state_now + fresh_state, None)


def in_blocks(operand):
    return operand.reshape(operand.shape[0] // SPAN, SPAN, operand.shape[1])


def ssd_run(inputs, writes, reading, decays, start_state):
    row_count = decays.shape[0]
    final_state, outputs = lax.scan(
        block_scan,
        start_state,
        (in_blocks(inputs), in_blocks(writes), in_blocks(reading), in_blocks(decays)),
    )
    return (outputs.reshape(row_count, outputs.shape[2]), final_state)


def gate_norm(ssd_out, inputs, gate_values, skip_gain, norm_gain):
    row_count = ssd_out.shape[0]
    head_count = skip_gain.shape[0]
    direct = (inputs.reshape(row_count, head_count, P_SIZE) * skip_gain[:, None]).reshape(
        row_count, head_count * P_SIZE
    )
    gated_vals = (ssd_out + direct) * jax.nn.silu(gate_values)
    grouped = gated_vals.reshape(row_count, -1, HALF_HEADS * P_SIZE // G)
    factor = lax.rsqrt(jnp.mean(grouped * grouped, axis=2, keepdims=True) + epsilon)
    return (grouped * factor).reshape(row_count, head_count * P_SIZE) * norm_gain


def combine(earlier, later):
    return (earlier[0] * later[0], later[0][..., None, None] * earlier[1] + later[1])


def per_device(
    ssd_input,
    gate_input,
    write_vectors,
    read_vectors,
    log_decay,
    skip_gain,
    norm_gain,
    out_weight,
    out_grad,
):
    row_count, head_count = log_decay.shape
    group_count = write_vectors.shape[1] // N
    per_group = head_count // group_count
    inputs = ssd_input.astype(jnp.float32)
    gate_values = gate_input.astype(jnp.float32)
    writes = write_vectors.astype(jnp.float32)
    reading = read_vectors.astype(jnp.float32)
    zero_state = jnp.zeros((group_count, per_group, P_SIZE, N), jnp.float32)
    own_state, unused = lax.scan(
        block_end, zero_state, (in_blocks(inputs), in_blocks(writes), in_blocks(log_decay))
    )
    cumulative = jnp.cumsum(log_decay, axis=0)
    own_decay = jnp.exp(cumulative[-1]).reshape(group_count, per_group)
    identity_pair = (jnp.ones_like(own_decay), zero_state)
    decay_before, start_state = entering((own_decay, own_state), "seq", combine, identity_pair)
    (ssd_out, end_state), ssd_pull = jax.vjp(
        ssd_run, inputs, writes, reading, log_decay, start_state
    )
    norm_fn = partial(gate_norm, skip_gain=skip_gain, norm_gain=norm_gain)
    normed, norm_pull = jax.vjp(norm_fn, ssd_out, inputs, gate_values)
    normed_half = normed.astype(jnp.bfloat16)
    partial_out = jnp.einsum(
        "th,dh->td", normed_half, out_weight, preferred_element_type=jnp.float32
    )
    layer_out = lax.psum_scatter(
        partial_out.astype(jnp.bfloat16), "head", scatter_dimension=1, tiled=True
    )
    full_grad = lax.all_gather(out_grad, "head", axis=1, tiled=True)
    normed_grad = jnp.dot(full_grad, out_weight, preferred_element_type=jnp.float32)
    ssd_grad, skip_input_grad, gate_grad = norm_pull(normed_grad)
    scaled_grad = ssd_grad.reshape(row_count, group_count, per_group, P_SIZE) * jnp.exp(
        cumulative
    ).reshape(row_count, group_count, per_group, 1)
    state_direct = jnp.einsum(
        "tgkp,tgn->gkpn", scaled_grad, reading.reshape(row_count, group_count, N), precision=highest
    )
    decay_after, end_grad = prefix((own_decay, state_direct), "seq", combine, identity_pair)
    input_part, write_grad, read_grad, decay_grad, start_grad = ssd_pull((ssd_grad, end_grad))
    input_grad = skip_input_grad + input_part
    weight_grad = lax.psum_scatter(
        jnp.einsum("td,th->dh", full_grad, normed_half, preferred_element_type=jnp.float32).astype(
            jnp.bfloat16
        ),
        "seq",
        scatter_dimension=0,
        tiled=True,
    )
    return (
        layer_out,
        input_grad.astype(jnp.bfloat16),
        gate_grad.astype(jnp.bfloat16),
        write_grad.astype(jnp.bfloat16),
        read_grad.astype(jnp.bfloat16),
        decay_grad,
        weight_grad,
    )


def solution(mesh):
    in_specs = (
        P("seq", "head"),
        P("seq", "head"),
        P("seq", "head"),
        P("seq", "head"),
        P("seq", "head"),
        P("head"),
        P("head"),
        P(None, "head"),
        P("seq", "head"),
    )
    out_specs = (
        P("seq", "head"),
        P("seq", "head"),
        P("seq", "head"),
        P("seq", "head"),
        P("seq", "head"),
        P("seq", "head"),
        P("seq", "head"),
    )
    return jax.shard_map(
        per_device, mesh=mesh, in_specs=in_specs, out_specs=out_specs, check_vma=False
    )
```

profile of v0, /device:TPU:0, one launch (start us, length us, event | category | flops | bytes accessed | tf_op | source)
XLA Modules:
  0.0 371.8 jit_solution(9372774571119833372)
XLA Ops:
  7.2 0.8 copy_bitcast_fusion.1
  10.6 1.4 fusion.30
  12.1 0.7 all-gather.8.cloned.1.call-update
  12.8 1.0 copy.126
  14.7 1.3 copy.135
  16.0 21.1 %all-gather.3 = bf16[16,1,16]{2,1,0:T(2,128)(2,1)S(1)} all-gather(bf16[1,1,16]{2,1,0:T(2,128)(2,1)S(1)} %get-tuple-element.601), channel_id=2, replica_groups=mesh['seq'=16,'head'=8] {'seq'}, dimensions={0}, use_global_device_ids=true | all-gather | bytes 544 | tf_op jit(solution)/shard_map/all_gather | solution.py:22
  37.4 47.9 %all-gather.10.cloned.1.call-done = bf16[256,64,256]{2,1,0:T(8,128)(2,1)} async-done(((bf16[16,64,256]{2,1,0:T(8,128)(2,1)}), bf16[256,64,256]{2,1,0:T(8,128)(2,1)}) %all-gather.10.cloned.1.call-update) | async-done | bytes 8388624 | tf_op jit(solution)/shard_map/all_gather | solution.py:22
  86.5 4.5 %fusion.24 = f32[256,1,16,64]{0,3,2,1:T(8,128)} fusion(bf16[256,16,64]{0,2,1:T(8,128)(2,1)S(1)} %bitcast.196, f32[16,256]{1,0:T(8,128)S(1)} %copy-done.18, f32[256,256]{1,0:T(8,128)S(1)} %fusion.61, pred[256,256]{1,0:T(8,128)(4,1)S(1)} %iota_compare_fusion, f32[256,1,16,64]{0,3,2,1:T(8,128)S(1)} %convolution_bitcast_fusion.1, f32[256,16]{0,1:T(8,128)S(1)} %copy.128), kind=kOutput, calls=%fused_computation.36 | convolution fusion | flops 810024960 | bytes 2981888 | tf_op jit(solution)/shard_map/jvp()/while/body/eval_jaxpr/gkts,sgkp->tgkp/dot_general | solution.py:80
  91.0 1.6 copy.133
  92.6 26.5 %all-gather.8.cloned.1.call-done = bf16[256,8192]{1,0:T(8,128)(2,1)} async-done(((bf16[256,1024]{1,0:T(8,128)(2,1)}), bf16[256,8192]{1,0:T(8,128)(2,1)}) %all-gather.8.cloned.1.call-update) | async-done | bytes 4194320 | tf_op jit(solution)/shard_map/all_gather | solution.py:171
  119.0 12.8 %multiply_reduce_fusion.4 = (f32[256]{0:T(256)S(1)}, f32[256]{0:T(256)S(1)}, f32[256,1024]{1,0:T(8,128)}, f32[256,1024]{1,0:T(8,128)S(1)}) fusion(bf16[256,1024]{1,0:T(8,128)(2,1)S(1)} %copy-done.11, f32[256,1024]{1,0:T(8,128)S(1)} %copy.133, f32[1024]{0:T(1024)} %mul.443, bf16[256,1024]{1,0:T(8,128)(2,1)S(1)} %copy-done.3, f32[1024]{0:T(1024)} %param.19, ...), kind=kOutput, calls=%fused_computation.64 | convolution fusion | flops 4298637312 | bytes 25176064 | tf_op jit(solution)/shard_map/dot_general | solution.py:172
  131.8 3.5 fusion.58
  135.4 2.6 copy.136
  137.9 2.6 convolution_convert_fusion.1
  140.8 13.3 %convert_bitcast_fusion = bf16[8192,1024]{0,1:T(8,128)(2,1)} fusion(bf16[256,8192]{1,0:T(8,128)(2,1)} %all-gather.8.cloned.1.call-done, f32[256,1024]{1,0:T(8,128)} %get-tuple-element.594, f32[1024]{0:T(1024)S(1)} %copy-done.14, f32[256]{0:T(256)S(1)} %copy-done.23), kind=kOutput, calls=%fused_computation.4 | convolution fusion | flops 4304142336 | bytes 22025216 | tf_op jit(solution)/shard_map/td,th->dh/dot_general | solution.py:184
  154.2 10.0 %convolution_convert_fusion = bf16[256,8192]{1,0:T(8,128)(2,1)} fusion(bf16[8192,1024]{1,0:T(8,128)(2,1)} %param.20, f32[256,1024]{1,0:T(8,128)} %get-tuple-element.594, f32[1024]{0:T(1024)S(1)} %copy-done.14, f32[256]{0:T(256)S(1)} %copy-done.23), kind=kOutput, calls=%fused_computation.5 | convolution fusion | flops 4297850880 | bytes 22025216 | tf_op jit(solution)/shard_map/th,dh->td/dot_general | solution.py:165
  164.2 1.2 copy.142
  165.8 6.6 %fusion.7 = (f32[16,256]{1,0:T(8,128)}, f32[16,256]{1,0:T(8,128)}, f32[256,256]{1,0:T(8,128)}) fusion(f32[16,256]{1,0:T(8,128)} %copy-done.17, f32[256,256]{1,0:T(8,128)} %copy-done.13, pred[256,256]{1,0:T(8,128)(4,1)} %copy-done.19, f32[16,64,256]{2,1,0:T(8,128)S(1)} %bitcast.177, bf16[256,16,64]{0,2,1:T(8,128)(2,1)} %bitcast.195), kind=kOutput, calls=%fused_computation.14 | convolution fusion | flops 816766976 | bytes 2211840 | tf_op jit(solution)/shard_map/transpose(jvp())/while/body/eval_jaxpr/gkts,sgkp->tgkp/dot_general | solution.py:80
  172.4 1.5 copy.146
  173.8 2.3 multiply_reduce_fusion.1
  176.1 1.5 copy.145
  177.6 1.5 copy.147
  179.1 2.0 convolution_bitcast_fusion.2
  181.0 1.8 convolution_bitcast_fusion.3
  182.9 1.6 fusion.57
  184.4 1.7 negate_add_fusion
  186.1 1.9 fusion.33
  188.0 23.3 %all-gather.12.cloned.1.call-done = bf16[256,64,256]{2,1,0:T(8,128)(2,1)} async-done(((bf16[16,64,256]{2,1,0:T(8,128)(2,1)}), bf16[256,64,256]{2,1,0:T(8,128)(2,1)}) %all-gather.12.cloned.1.call-update) | async-done | bytes 8388624 | tf_op jit(solution)/shard_map/all_gather | solution.py:44
  211.4 29.8 %while.21 = (s32[]{:T(128)}, f32[1,16,64,256]{3,2,1,0:T(8,128)S(1)}, s32[]{:T(128)}, bf16[16,1,16]{2,1,0:T(2,128)(2,1)}, bf16[16,1,16,64,256]{4,3,2,1,0:T(8,128)...) while((s32[]{:T(128)}, f32[1,16,64,256]{3,2,1,0:T(8,128)S(1)}, s32[]{:T(128)}, ...), condition=%wide.region_8.9_spmd, body=%wide.region_7.8_spmd.sunk | while | flops 786454 | bytes 2621755 | solution.py:61
  212.2 1.3 convert_add_fusion.5
  214.1 1.3 convert_add_fusion.5
  216.0 1.3 convert_add_fusion.5
  218.0 1.3 convert_add_fusion.5
  219.3 0.7 bitcast_convert_fusion.5
  220.0 1.3 convert_add_fusion.5
  221.3 0.7 bitcast_convert_fusion.5
  222.0 1.3 convert_add_fusion.5
  223.3 0.7 bitcast_convert_fusion.5
  224.0 1.3 convert_add_fusion.5
  226.0 1.3 convert_add_fusion.5
  228.0 1.3 convert_add_fusion.5
  229.3 0.7 bitcast_convert_fusion.5
  230.0 1.3 convert_add_fusion.5
  231.9 1.3 convert_add_fusion.5
  233.9 1.3 convert_add_fusion.5
  235.2 0.7 bitcast_convert_fusion.5
  235.9 1.3 convert_add_fusion.5
  237.9 1.3 convert_add_fusion.5
  239.2 0.7 bitcast_convert_fusion.5
  239.9 1.3 convert_add_fusion.5
  241.2 3.0 multiply_reduce_fusion.3
  244.2 0.8 copy.143
  245.0 6.6 %fusion.27 = f32[256,1,16,64]{0,3,2,1:T(8,128)} fusion(f32[16,64,256]{2,1,0:T(8,128)} %bitcast.180, f32[16,256]{1,0:T(8,128)} %copy-done.17, f32[256,256]{1,0:T(8,128)} %copy-done.13, pred[256,256]{1,0:T(8,128)(4,1)} %copy-done.19, f32[256,1,16,64]{0,3,2,1:T(8,128)} %get-tuple-element.607, f32[256,16]{0,1:T(8,128)S(1)} %copy-done.16), kind=kOutput, calls=%fused_computation.37 | convolution fusion | flops 810024960 | bytes 3506176 | tf_op jit(solution)/shard_map/transpose(jvp())/while/body/eval_jaxpr/gkts,sgkp->tgkp/dot_general | solution.py:80
  251.6 2.6 copy.140
  254.4 1.1 multiply_reduce_fusion.6
  255.5 1.2 add_add_fusion.1
  256.7 2.5 reduce-window.36
  259.3 3.2 fusion.34
  262.5 0.8 copy.150
  263.3 0.7 bitcast_bitcast_fusion
  264.0 1.0 add_convert_fusion
  265.0 59.9 %reduce-scatter.5.cloned.1.call-done = bf16[512,1024]{0,1:T(8,128)(2,1)} async-done(((bf16[8192,1024]{0,1:T(8,128)(2,1)}), bf16[512,1024]{0,1:T(8,128)(2,1)}) %reduce-scatter.5.cloned.1.call-update) | async-done | bytes 1048592 | tf_op jit(solution)/shard_map/reduce_scatter | solution.py:183
  324.9 2.3 copy.151
  327.2 38.1 %reduce-scatter.3.cloned.1.call-done = bf16[256,1024]{1,0:T(8,128)(2,1)} async-done(((bf16[256,8192]{1,0:T(8,128)(2,1)}), bf16[256,1024]{1,0:T(8,128)(2,1)}) %reduce-scatter.3.cloned.1.call-update) | async-done | bytes 524304 | tf_op jit(solution)/shard_map/reduce_scatter | solution.py:168
  (101 shorter events, 11.6 us)
Async XLA Ops:
  7.2 3.4 copy-start
  7.2 2.9 copy-start.3
  7.2 78.1 %all-gather.10.cloned.1.call-start = ((), (), s32[]{:S(2)}) async-start(), calls=%async_computation.5 | async-start | bytes 8912896 | tf_op jit(solution)/shard_map/all_gather | solution.py:22
  8.9 0.6 copy-start.17
  9.5 2.5 copy-start.9
  9.6 2.4 copy-start.15
  10.0 3.8 %copy-start.25 = (f32[16]{0:T(128)S(1)}, f32[16]{0:T(128)}, u32[]{:S(2)}) copy-start(f32[16]{0:T(128)} %param.18) | copy-start | bytes 196
  10.2 26.9 %copy-start.8 = (bf16[256,256]{1,0:T(8,128)(2,1)S(1)}, bf16[256,256]{1,0:T(8,128)(2,1)}, u32[]{:S(2)}) copy-start(bf16[256,256]{1,0:T(8,128)(2,1)} %param.16) | copy-start | bytes 393220
  10.5 74.8 %copy-start.1 = (f32[256,1024]{0,1:T(8,128)}, f32[256,1024]{0,1:T(8,128)S(1)}, u32[]{:S(2)}) copy-start(f32[256,1024]{0,1:T(8,128)S(1)} %copy.131) | copy-start | bytes 3145732
  12.0 107.0 %all-gather.8.cloned.1.call-start = ((), (), s32[]{:S(2)}) async-start(), calls=%async_computation.3 | async-start | bytes 4718592 | tf_op jit(solution)/shard_map/all_gather | solution.py:171
  12.8 198.5 %all-gather.12.cloned.1.call-start = ((), (), s32[]{:S(2)}) async-start(), calls=%async_computation.6 | async-start | bytes 8912896 | tf_op jit(solution)/shard_map/all_gather | solution.py:44
  37.1 49.0 %copy-start.19 = (pred[256,256]{1,0:T(8,128)(4,1)}, pred[256,256]{1,0:T(8,128)(4,1)S(1)}, u32[]{:S(2)}) copy-start(pred[256,256]{1,0:T(8,128)(4,1)S(1)} %iota_compare_fusion) | copy-start | bytes 196612
  37.4 48.8 %copy-start.13 = (f32[256,256]{1,0:T(8,128)}, f32[256,256]{1,0:T(8,128)S(1)}, u32[]{:S(2)}) copy-start(f32[256,256]{1,0:T(8,128)S(1)} %fusion.61) | copy-start | bytes 786436
  85.4 1.1 copy-start.12
  85.4 1.0 copy-start.18
  85.5 5.5 %copy-start.24 = (bf16[16,1,16]{2,1,0:T(2,128)(2,1)}, bf16[16,1,16]{2,1,0:T(2,128)(2,1)S(1)}, u32[]{:S(2)}) copy-start(bf16[16,1,16]{2,1,0:T(2,128)(2,1)S(1)} %get-tuple-element.742) | copy-start | bytes 1540
  86.1 4.9 %copy-start.7 = (f32[256,1,16,64]{0,3,2,1:T(8,128)}, f32[256,1,16,64]{0,3,2,1:T(8,128)S(1)}, u32[]{:S(2)}) copy-start(f32[256,1,16,64]{0,3,2,1:T(8,128)S(1)} %convolution_bitcast_fusion.1) | copy-start | bytes 3145732
  86.5 32.5 %copy-start.11 = (bf16[256,1024]{1,0:T(8,128)(2,1)S(1)}, bf16[256,1024]{1,0:T(8,128)(2,1)}, u32[]{:S(2)}) copy-start(bf16[256,1024]{1,0:T(8,128)(2,1)} %param.14) | copy-start | bytes 1572868
  92.6 39.2 %copy-start.6 = (f32[256,1024]{1,0:T(8,128)}, f32[256,1024]{1,0:T(8,128)S(1)}, u32[]{:S(2)}) copy-start(f32[256,1024]{1,0:T(8,128)S(1)} %copy.133) | copy-start | bytes 3145732
  119.0 12.8 %copy-start.4 = (f32[256,1024]{1,0:T(8,128)S(1)}, f32[256,1024]{1,0:T(8,128)}, u32[]{:S(2)}) copy-start(f32[256,1024]{1,0:T(8,128)} %copy.135) | copy-start | bytes 3145732
  119.0 12.8 %copy-start.20 = (f32[1024]{0:T(1024)S(1)}, f32[1024]{0:T(1024)}, u32[]{:S(2)}) copy-start(f32[1024]{0:T(1024)} %mul.443) | copy-start | bytes 12292
  131.8 3.5 copy-start.22
  135.4 5.5 %copy-start.14 = (f32[1024]{0:T(1024)S(1)}, f32[1024]{0:T(1024)}, u32[]{:S(2)}) copy-start(f32[1024]{0:T(1024)} %param.19) | copy-start | bytes 12292
  135.4 5.5 %copy-start.23 = (f32[256]{0:T(256)S(1)}, f32[256]{0:T(256)}, u32[]{:S(2)}) copy-start(f32[256]{0:T(256)} %copy-done.22) | copy-start | bytes 3076
  140.6 184.3 %reduce-scatter.5.cloned.1.call-start = ((), (), s32[]{:S(2)}) async-start(), calls=%async_computation.4 | async-start | bytes 17825792 | tf_op jit(solution)/shard_map/reduce_scatter | solution.py:183
  154.1 211.1 %reduce-scatter.3.cloned.1.call-start = ((), (), s32[]{:S(2)}) async-start(), calls=%async_computation.2 | async-start | bytes 4718592 | tf_op jit(solution)/shard_map/reduce_scatter | solution.py:168
  165.8 15.2 %copy-start.2 = (f32[256,1024]{0,1:T(8,128)}, f32[256,1024]{0,1:T(8,128)S(1)}, u32[]{:S(2)}) copy-start(f32[256,1024]{0,1:T(8,128)S(1)} %copy.139) | copy-start | bytes 3145732
  211.4 33.6 %copy-start.16 = (f32[256,16]{0,1:T(8,128)S(1)}, f32[256,16]{0,1:T(8,128)}, u32[]{:S(2)}) copy-start(f32[256,16]{0,1:T(8,128)} %copy-done.15) | copy-start | bytes 49156
  245.0 9.4 %copy-start.10 = (f32[256,16]{1,0:T(8,128)S(1)}, f32[256,16]{1,0:T(8,128)}, u32[]{:S(2)}) copy-start(f32[256,16]{1,0:T(8,128)} %copy-done.9) | copy-start | bytes 49156
  251.6 12.4 %copy-start.21 = (f32[1024]{0:T(1024)S(1)}, f32[1024]{0:T(1024)}, u32[]{:S(2)}) copy-start(f32[1024]{0:T(1024)} %mul.443) | copy-start | bytes 12292
  254.4 9.6 %copy-start.5 = (f32[256,1024]{1,0:T(8,128)S(1)}, f32[256,1024]{1,0:T(8,128)}, u32[]{:S(2)}) copy-start(f32[256,1024]{1,0:T(8,128)} %copy.140) | copy-start | bytes 3145732
Sparse Core Ops, SparseCore 0:
  12.1 73.1 all-gather.9
  87.0 31.9 all-gather.7
  140.7 70.4 all-gather.11
  214.5 110.3 reduce-scatter.4
  327.7 37.4 reduce-scatter.2
where the time goes:
time: 374 us; the launch traced here: 372 us
  waiting for transfers between devices  196 us (52%)
  matrix products  70.5 us (19%)
  other arithmetic  45.8 us (12%)
  local copies, waits for them, and re-layouts  22.8 us (6%)
  blocking collectives  21.1 us (6%)
  between operations  14.1 us (4%)
    reduce_scatter x1, waiting for transfers between devices, per_device(): lax.psum_scatter(jnp.einsum('td,th->dh', full_grad, normed_half, preferre...  59.9 us
    all_gather x1, waiting for transfers between devices, entering(): lax.all_gather(a.astype(kind), axis)  47.9 us
    reduce_scatter x1, waiting for transfers between devices, per_device(): lax.psum_scatter(partial_out.astype(jnp.bfloat16), 'head', scatter_dimens...  38.1 us
    all_gather x1, waiting for transfers between devices, per_device(): full_grad = lax.all_gather(out_grad, 'head', axis=1, tiled=True)  26.5 us
    all_gather x1, waiting for transfers between devices, prefix(): lax.all_gather(a.astype(kind), axis)  23.3 us
    all_gather x1, blocking collectives, entering(): lax.all_gather(a.astype(kind), axis)  21.1 us
    add x15, other arithmetic, combine(): later[0][..., None, None] * earlier[1] + later[1]  19.6 us
    dot_general x3, matrix products, block_scan(): jnp.einsum('gkts,sgkp->tgkp', weights, input_heads, precision=highest)  17.7 us
  transfers between devices with their start and end apart: 5, of which 5 were waited for; matrix products, arithmetic and copies ran while one was open for 30% of the time, Pallas kernels for 0%

commit v1 on v0

--- a/solution.py
+++ b/solution.py
@@ -16,49 +16,29 @@
 highest = lax.Precision.HIGHEST
 
 
-def entering(x, axis, join, neutral):
-    place = lax.axis_index(axis)
-    gathered = jax.tree.map(
-        lambda a, kind: lax.all_gather(a.astype(kind), axis), x, (jnp.bfloat16, jnp.bfloat16)
-    )
-    state = jax.tree.map(lambda a, e: jnp.zeros_like(a) + jnp.asarray(e, a.dtype), x, neutral)
-
-    def entering_one(hop, state):
-        return join(
-            state,
-            jax.tree.map(
-                lambda a, own: lax.dynamic_index_in_dim(a, hop, 0, False).astype(own.dtype),
-                gathered,
-                x,
-            ),
-        )
-
-    return lax.fori_loop(0, place, entering_one, state)
-
-
-def prefix(x, axis, join, neutral):
+def log_scan(x, axis, reverse):
     count = lax.axis_size(axis)
     place = lax.axis_index(axis)
-    ahead = count - 1 - place
-    gathered = jax.tree.map(
-        lambda a, kind: lax.all_gather(a.astype(kind), axis),
-        x,
-        jax.tree.map(lambda a: jnp.bfloat16 if a.dtype == jnp.float32 else a.dtype, x),
-    )
-    state = jax.tree.map(lambda a, e: jnp.zeros_like(a) + jnp.asarray(e, a.dtype), x, neutral)
-
-    def prefix_one(hop, state):
-        source = count - 1 - hop
-        return join(
-            state,
-            jax.tree.map(
-                lambda a, own: lax.dynamic_index_in_dim(a, source, 0, False).astype(own.dtype),
-                gathered,
-                x,
-            ),
-        )
-
-    return lax.fori_loop(0, ahead, prefix_one, state)
+    decay, state = x
+    incl = (decay, state)
+    excl = (jnp.ones_like(decay), jnp.zeros_like(state))
+    hop = 1
+    while hop < count:
+        if reverse:
+            pairs = [(i + hop, i) for i in range(count - hop)]
+            valid = place + hop < count
+        else:
+            pairs = [(i, i + hop) for i in range(count - hop)]
+            valid = place >= hop
+        got_decay = lax.ppermute(incl[0], axis, pairs)
+        got_state = lax.ppermute(incl[1].astype(jnp.bfloat16), axis, pairs).astype(jnp.float32)
+        got_decay = jnp.where(valid, got_decay, 1.0)
+        got_state = jnp.where(valid, got_state, 0.0)
+        excl = (got_decay * excl[0], excl[0][..., None, None] * got_state + excl[1])
+        if hop * 2 < count:
+            incl = (got_decay * incl[0], incl[0][..., None, None] * got_state + incl[1])
+        hop *= 2
+    return excl
 
 
 def block_scan(state_now, pieces):
@@ -154,8 +134,7 @@
     )
     cumulative = jnp.cumsum(log_decay, axis=0)
     own_decay = jnp.exp(cumulative[-1]).reshape(group_count, per_group)
-    identity_pair = (jnp.ones_like(own_decay), zero_state)
-    decay_before, start_state = entering((own_decay, own_state), "seq", combine, identity_pair)
+    decay_before, start_state = log_scan((own_decay, own_state), "seq", False)
     (ssd_out, end_state), ssd_pull = jax.vjp(
         ssd_run, inputs, writes, reading, log_decay, start_state
     )
@@ -177,7 +156,7 @@
     state_direct = jnp.einsum(
         "tgkp,tgn->gkpn", scaled_grad, reading.reshape(row_count, group_count, N), precision=highest
     )
-    decay_after, end_grad = prefix((own_decay, state_direct), "seq", combine, identity_pair)
+    decay_after, end_grad = log_scan((own_decay, state_direct), "seq", True)
     input_part, write_grad, read_grad, decay_grad, start_grad = ssd_pull((ssd_grad, end_grad))
     input_grad = skip_input_grad + input_part
     weight_grad = lax.psum_scatter(

time: 374 us -> 320 us (0.86)
  waiting for transfers between devices: 196 us -> 122 us
  starting transfers between devices: 0.38 us -> 48.1 us
  blocking collectives: 21.1 us -> 0 us
  other arithmetic: 45.8 us -> 41.1 us
    ppermute x0 -> x14, waiting for transfers between devices: none -> 101 us  [the longest x8 72.7 us: log_scan(): lax.ppermute(incl[1].astype(jnp.bfloat16), axis, pairs).astype(jnp.float32)]
    all_gather x2 -> x0, waiting for transfers between devices: 71.2 us -> none  [the longest x1 47.9 us: entering(): lax.all_gather(a.astype(kind), axis)]
    reduce_scatter x1, waiting for transfers between devices: 59.9 us -> 0.01 us  [per_device(): lax.psum_scatter(jnp.einsum('td,th->dh', full_grad, normed_half, preferre...]
    ppermute x0 -> x14, starting transfers between devices: none -> 47.7 us  [the longest x8 34.9 us: log_scan(): lax.ppermute(incl[1].astype(jnp.bfloat16), axis, pairs).astype(jnp.float32)]
    all_gather x1, waiting for transfers between devices: 26.5 us -> 0.01 us  [per_device(): full_grad = lax.all_gather(out_grad, 'head', axis=1, tiled=True)]
    all_gather x1 -> x0, blocking collectives: 21.1 us -> none  [entering(): lax.all_gather(a.astype(kind), axis)]
    add x15 -> x1, other arithmetic: 19.6 us -> 1.88 us  [log_scan(): excl = (got_decay * excl[0], excl[0][..., None, None] * got_state + excl[1])]
    reduce_scatter x1, waiting for transfers between devices: 38.1 us -> 20.6 us  [per_device(): lax.psum_scatter(partial_out.astype(jnp.bfloat16), 'head', scatter_dimens...]
  transfers between devices with their start and end apart: 5 -> 17, of which waited for: 5 -> 12; matrix products, arithmetic and copies ran while one was open for 30% -> 34% of each run, Pallas kernels for 0% -> 0%
where the time goes in v1:
time: 320 us; the launch traced here: 318 us
  waiting for transfers between devices  122 us (38%)
  matrix products  67.1 us (21%)
  starting transfers between devices  48.1 us (15%)
  other arithmetic  41.1 us (13%)
  local copies, waits for them, and re-layouts  25.5 us (8%)
  between operations  14.2 us (4%)
    ppermute x8, waiting for transfers between devices, log_scan(): lax.ppermute(incl[1].astype(jnp.bfloat16), axis, pairs).astype(jnp.float32)  72.7 us
    ppermute x8, starting transfers between devices, log_scan(): lax.ppermute(incl[1].astype(jnp.bfloat16), axis, pairs).astype(jnp.float32)  34.9 us
    ppermute x6, waiting for transfers between devices, log_scan(): got_decay = lax.ppermute(incl[0], axis, pairs)  28.2 us
    reduce_scatter x1, waiting for transfers between devices, per_device(): lax.psum_scatter(partial_out.astype(jnp.bfloat16), 'head', scatter_dimens...  20.6 us
    dot_general x3, matrix products, block_scan(): jnp.einsum('gkts,sgkp->tgkp', weights, input_heads, precision=highest)  17.5 us
    dot_general x1, matrix products, per_device(): jnp.dot(full_grad, out_weight, preferred_element_type=jnp.float32)  12.9 us
    ppermute x6, starting transfers between devices, log_scan(): got_decay = lax.ppermute(incl[0], axis, pairs)  12.8 us
    convert_element_type x8, other arithmetic, log_scan(): incl[1].astype(jnp.bfloat16)  12 us
  transfers between devices with their start and end apart: 17, of which 12 were waited for; matrix products, arithmetic and copies ran while one was open for 34% of the time, Pallas kernels for 0%

profile of v1, /device:TPU:0, one launch (start us, length us, event | category | flops | bytes accessed | tf_op | source)
XLA Modules:
  0.0 318.3 jit_solution(11093234797980219534)
XLA Ops:
  9.7 1.3 collective-permute-start.7
  11.0 4.5 %collective-permute-start = (f32[1,16]{1,0:T(1,128)S(1)}, f32[1,16]{1,0:T(1,128)S(1)}, u32[]{:S(2)}, u32[]{:S(2)}) collective-permute-start(f32[1,16]{1,0:T(1,128)S(1)} %slice_exponential_fusion), channel_id=1, source_target_pairs={{0,8},{8,16},{16,24},{24,32},{32,40},{40,48},{48,56},{56,64},{64,7... | collective-permute-start | bytes 200 | tf_op jit(solution)/shard_map/ppermute | solution.py:33
  15.5 1.3 collective-permute-done
  18.6 1.1 convert_multiply_fusion.2
  19.7 1.6 copy.102
  22.0 4.2 %collective-permute-start.3 = (bf16[1,16,64,256]{3,2,1,0:T(8,128)(2,1)S(1)}, bf16[1,16,64,256]{3,2,1,0:T(8,128)(2,1)S(1)}, u32[]{:S(2)}, u32[]{:S(2)}) collective-permute-start(bf16[1,16,64,256]{3,2,1,0:T(8,128)(2,1)S(1)} %convert_bitcast_fusion.2), channel_id=1, source_target_pairs={{0,8},{8,16},{16,24},{24,32},{32,40},{40,48},{48,56},{56,64},{64,7... | collective-permute-start | bytes 1572872 | tf_op jit(solution)/shard_map/ppermute | solution.py:34
  26.3 9.6 %collective-permute-done.3 = bf16[1,16,64,256]{3,2,1,0:T(8,128)(2,1)S(1)} collective-permute-done((bf16[1,16,64,256]{3,2,1,0:T(8,128)(2,1)S(1)}, bf16[1,16,64,256]{3,2,1,0:T(8,128)(2,1)S(1)}, u32[]{:S(2)}, u32[]{:S(2)}) %collective-permute-start.3) | collective-permute-done | bytes 524320 | tf_op jit(solution)/shard_map/ppermute | solution.py:34
  35.9 1.0 fusion.73
  36.8 7.5 %collective-permute-start.4 = (bf16[1,16,64,256]{3,2,1,0:T(8,128)(2,1)}, bf16[1,16,64,256]{3,2,1,0:T(8,128)(2,1)}, u32[]{:S(2)}, u32[]{:S(2)}) collective-permute-start(bf16[1,16,64,256]{3,2,1,0:T(8,128)(2,1)} %fusion.73), channel_id=1, source_target_pairs={{0,16},{8,24},{16,32},{24,40},{32,48},{40,56},{48,64},{56,72},{64,... | collective-permute-start | bytes 1572872 | tf_op jit(solution)/shard_map/ppermute | solution.py:34
  44.4 8.6 %collective-permute-done.4 = bf16[1,16,64,256]{3,2,1,0:T(8,128)(2,1)} collective-permute-done((bf16[1,16,64,256]{3,2,1,0:T(8,128)(2,1)}, bf16[1,16,64,256]{3,2,1,0:T(8,128)(2,1)}, u32[]{:S(2)}, u32[]{:S(2)}) %collective-permute-start.4) | collective-permute-done | bytes 524320 | tf_op jit(solution)/shard_map/ppermute | solution.py:34
  53.0 2.2 fusion.46
  55.2 11.8 %collective-permute-start.5 = (bf16[1,16,64,256]{3,2,1,0:T(8,128)(2,1)}, bf16[1,16,64,256]{3,2,1,0:T(8,128)(2,1)}, u32[]{:S(2)}, u32[]{:S(2)}) collective-permute-start(bf16[1,16,64,256]{3,2,1,0:T(8,128)(2,1)} %fusion.46), channel_id=1, source_target_pairs={{0,32},{8,40},{16,48},{24,56},{32,64},{40,72},{48,80},{56,88},{64,... | collective-permute-start | bytes 1572872 | tf_op jit(solution)/shard_map/ppermute | solution.py:34
  67.0 1.0 copy.97
  68.0 1.5 collective-permute-start.1
  70.7 3.8 %collective-permute-done.5 = bf16[1,16,64,256]{3,2,1,0:T(8,128)(2,1)} collective-permute-done((bf16[1,16,64,256]{3,2,1,0:T(8,128)(2,1)}, bf16[1,16,64,256]{3,2,1,0:T(8,128)(2,1)}, u32[]{:S(2)}, u32[]{:S(2)}) %collective-permute-start.5) | collective-permute-done | bytes 524320 | tf_op jit(solution)/shard_map/ppermute | solution.py:34
  74.5 1.7 add_convert_fusion.2
  76.2 6.0 %collective-permute-start.6 = (bf16[1,16,64,256]{3,2,1,0:T(8,128)(2,1)S(1)}, bf16[1,16,64,256]{3,2,1,0:T(8,128)(2,1)S(1)}, u32[]{:S(2)}, u32[]{:S(2)}) collective-permute-start(bf16[1,16,64,256]{3,2,1,0:T(8,128)(2,1)S(1)} %add_convert_fusion.2), channel_id=1, source_target_pairs={{0,64},{8,72},{16,80},{24,88},{32,96},{40,104},{48,112},{56,120},{... | collective-permute-start | bytes 1572872 | tf_op jit(solution)/shard_map/ppermute | solution.py:34
  83.8 3.0 collective-permute-start.2
  86.8 2.5 collective-permute-done.2
  90.8 1.9 add_add_fusion.2
  93.3 6.0 %fusion.24 = f32[256,1,16,64]{0,3,2,1:T(8,128)} fusion(bf16[256,16,64]{0,2,1:T(8,128)(2,1)} %bitcast.203, f32[16,256]{1,0:T(8,128)} %copy-done.21, f32[256,256]{1,0:T(8,128)S(1)} %copy-done.17, pred[256,256]{1,0:T(8,128)(4,1)S(1)} %copy-done.23, f32[256,1,16,64]{0,3,2,1:T(8,128)S(1)} %convolution_bitcast_fusion.1, f32[256,16]{0,1:T(8,128)S(1)} %copy.99), kind=kOutput, calls=%fused_computation.32 | convolution fusion | flops 810024960 | bytes 2981888 | tf_op jit(solution)/shard_map/jvp()/while/body/eval_jaxpr/gkts,sgkp->tgkp/dot_general | solution.py:60
  99.4 2.6 copy.103
  101.9 12.9 %multiply_reduce_fusion.4 = (f32[256]{0:T(256)S(1)}, f32[256]{0:T(256)S(1)}, f32[256,1024]{1,0:T(8,128)S(1)}, f32[256,1024]{1,0:T(8,128)}) fusion(bf16[256,1024]{1,0:T(8,128)(2,1)S(1)} %copy-done.12, f32[256,1024]{1,0:T(8,128)} %copy.103, f32[1024]{0:T(1024)} %mul.570, bf16[256,1024]{1,0:T(8,128)(2,1)S(1)} %copy-done.4, f32[1024]{0:T(1024)} %param.15, ...), kind=kOutput, calls=%fused_computation.66 | convolution fusion | flops 4298637312 | bytes 25176064 | tf_op jit(solution)/shard_map/dot_general | solution.py:151
  115.5 10.4 %convert_bitcast_fusion = bf16[8192,1024]{0,1:T(8,128)(2,1)} fusion(bf16[256,8192]{1,0:T(8,128)(2,1)} %all-gather.2.cloned.1.call-done, f32[256,1024]{1,0:T(8,128)S(1)} %get-tuple-element.381, f32[1024]{0:T(1024)} %param.15, f32[256]{0:T(256)} %get-tuple-element.396), kind=kOutput, calls=%fused_computation | convolution fusion | flops 4304142336 | bytes 22025216 | tf_op jit(solution)/shard_map/td,th->dh/dot_general | solution.py:163
  126.2 9.6 %convolution_convert_fusion = bf16[256,8192]{1,0:T(8,128)(2,1)} fusion(bf16[8192,1024]{1,0:T(8,128)(2,1)} %param.16, f32[256,1024]{1,0:T(8,128)S(1)} %get-tuple-element.381, f32[1024]{0:T(1024)} %param.15, f32[256]{0:T(256)} %get-tuple-element.396), kind=kOutput, calls=%fused_computation.1 | convolution fusion | flops 4297850880 | bytes 22025216 | tf_op jit(solution)/shard_map/th,dh->td/dot_general | solution.py:144
  135.9 1.3 copy.105
  137.2 4.1 %fusion.75 = (f32[256,1024]{1,0:T(8,128)}, f32[256,1024]{1,0:T(8,128)S(1)}, bf16[256,1024]{1,0:T(8,128)(2,1)}) fusion(f32[256,1024]{1,0:T(8,128)} %copy.105, bf16[256,1024]{1,0:T(8,128)(2,1)S(1)} %copy-done.12, f32[256,1024]{1,0:T(8,128)} %copy-done.5, f32[256]{0:T(256)} %get-tuple-element.395, f32[256,1024]{1,0:T(8,128)} %get-tuple-element.399, ...), kind=kLoop, calls=%fused_computation.135 | loop fusion | flops 5767168 | bytes 7870464 | tf_op jit(solution)/shard_map/mul | solution.py:153
  141.3 2.6 copy.106
  143.9 1.9 fusion.51
  146.7 1.3 collective-permute-start.10
  148.0 2.2 copy.111
  150.2 1.3 collective-permute-start.8
  151.5 5.8 %collective-permute-done.8 = f32[1,16]{1,0:T(1,128)} collective-permute-done((f32[1,16]{1,0:T(1,128)}, f32[1,16]{1,0:T(1,128)}, u32[]{:S(2)}, u32[]{:S(2)}) %collective-permute-start.8) | collective-permute-done | bytes 96 | tf_op jit(solution)/shard_map/ppermute | solution.py:33
  157.3 1.2 fusion.64
  158.5 1.3 collective-permute-start.9
  159.8 18.1 %collective-permute-done.9 = f32[1,16]{1,0:T(1,128)} collective-permute-done((f32[1,16]{1,0:T(1,128)}, f32[1,16]{1,0:T(1,128)}, u32[]{:S(2)}, u32[]{:S(2)}) %collective-permute-start.9) | collective-permute-done | bytes 96 | tf_op jit(solution)/shard_map/ppermute | solution.py:33
  177.9 1.3 fusion.60
  179.2 1.3 copy.108
  180.5 2.0 fusion.74
  182.5 1.3 collective-permute-start.11
  183.8 2.3 multiply_reduce_fusion.1
  186.1 1.5 copy.114
  187.6 3.9 %convolution_bitcast_fusion.3 = f32[256,256]{1,0:T(8,128)} fusion(f32[1,16,64,256]{3,2,1,0:T(8,128)S(1)} %add_add_fusion.2, f32[256,1,16,64]{0,3,2,1:T(8,128)} %bitcast.186, f32[256,16]{0,1:T(8,128)S(1)} %copy.99), kind=kOutput, calls=%fused_computation.36 | convolution fusion | flops 805568512 | bytes 2375680 | tf_op jit(solution)/shard_map/transpose(jvp())/while/body/eval_jaxpr/tgn,gkpn->tgkp/dot_general | solution.py:61
  191.5 1.6 fusion.72
  193.1 18.2 %collective-permute-done.11 = bf16[1,16,64,256]{3,2,1,0:T(8,128)(2,1)} collective-permute-done((bf16[1,16,64,256]{3,2,1,0:T(8,128)(2,1)}, bf16[1,16,64,256]{3,2,1,0:T(8,128)(2,1)}, u32[]{:S(2)}, u32[]{:S(2)}) %collective-permute-start.11) | collective-permute-done | bytes 524320 | tf_op jit(solution)/shard_map/ppermute | solution.py:34
  211.4 1.5 fusion.47
  212.9 1.3 collective-permute-start.12
  214.3 5.0 %fusion.7 = (f32[16,256]{1,0:T(8,128)}, f32[16,256]{1,0:T(8,128)S(1)}, f32[256,256]{1,0:T(8,128)S(1)}) fusion(f32[16,256]{1,0:T(8,128)S(1)} %copy-done.22, f32[256,256]{1,0:T(8,128)S(1)} %copy-done.18, pred[256,256]{1,0:T(8,128)(4,1)S(1)} %copy-done.24, f32[16,64,256]{2,1,0:T(8,128)S(1)} %bitcast.188, bf16[256,16,64]{0,2,1:T(8,128)(2,1)S(1)} %bitcast.204), kind=kOutput, calls=%fused_computation.10 | convolution fusion | flops 816766976 | bytes 2211840 | tf_op jit(solution)/shard_map/transpose(jvp())/while/body/eval_jaxpr/gkts,sgkp->tgkp/dot_general | solution.py:60
  219.3 18.9 %collective-permute-done.12 = bf16[1,16,64,256]{3,2,1,0:T(8,128)(2,1)S(1)} collective-permute-done((bf16[1,16,64,256]{3,2,1,0:T(8,128)(2,1)S(1)}, bf16[1,16,64,256]{3,2,1,0:T(8,128)(2,1)S(1)}, u32[]{:S(2)}, u32[]{:S(2)}) %collective-permute-start.12) | collective-permute-done | bytes 524320 | tf_op jit(solution)/shard_map/ppermute | solution.py:34
  238.2 2.7 add_convert_fusion.1
  240.9 1.5 collective-permute-start.13
  242.4 1.0 convolution_bitcast_fusion.2
  245.0 2.0 fusion.32
  247.0 13.6 %collective-permute-done.13 = bf16[1,16,64,256]{3,2,1,0:T(8,128)(2,1)S(1)} collective-permute-done((bf16[1,16,64,256]{3,2,1,0:T(8,128)(2,1)}, bf16[1,16,64,256]{3,2,1,0:T(8,128)(2,1)S(1)}, u32[]{:S(2)}, u32[]{:S(2)}) %collective-permute-start.13) | collective-permute-done | bytes 524320 | tf_op jit(solution)/shard_map/ppermute | solution.py:34
  261.4 2.8 multiply_reduce_fusion.2
  264.3 2.9 multiply_reduce_fusion.3
  267.9 6.5 %fusion.27 = f32[256,1,16,64]{0,3,2,1:T(8,128)} fusion(f32[16,64,256]{2,1,0:T(8,128)} %bitcast.187, f32[16,256]{1,0:T(8,128)} %copy-done.21, f32[256,256]{1,0:T(8,128)} %fusion.78, pred[256,256]{1,0:T(8,128)(4,1)} %iota_compare_fusion, f32[256,1,16,64]{0,3,2,1:T(8,128)} %get-tuple-element.401, f32[256,16]{0,1:T(8,128)S(1)} %copy-done.20), kind=kOutput, calls=%fused_computation.33 | convolution fusion | flops 810024960 | bytes 3506176 | tf_op jit(solution)/shard_map/transpose(jvp())/while/body/eval_jaxpr/gkts,sgkp->tgkp/dot_general | solution.py:60
  274.4 2.5 copy.109
  278.6 1.2 add_add_fusion.3
  279.8 2.5 reduce-window.36
  282.4 2.8 fusion.33
  286.7 2.2 add_convert_fusion
  288.9 2.3 copy.120
  291.2 20.6 %reduce-scatter.3.cloned.1.call-done = bf16[256,1024]{1,0:T(8,128)(2,1)} async-done(((bf16[256,8192]{1,0:T(8,128)(2,1)}), bf16[256,1024]{1,0:T(8,128)(2,1)}) %reduce-scatter.3.cloned.1.call-update) | async-done | bytes 524304 | tf_op jit(solution)/shard_map/reduce_scatter | solution.py:147
  (111 shorter events, 18.3 us)
Async XLA Ops:
  7.2 14.1 %copy-start = (bf16[256,256]{1,0:T(8,128)(2,1)S(1)}, bf16[256,256]{1,0:T(8,128)(2,1)}, u32[]{:S(2)}) copy-start(bf16[256,256]{1,0:T(8,128)(2,1)} %param.11) | copy-start | bytes 393220
  7.2 11.4 %copy-start.4 = (bf16[256,1024]{1,0:T(8,128)(2,1)S(1)}, bf16[256,1024]{1,0:T(8,128)(2,1)}, u32[]{:S(2)}) copy-start(bf16[256,1024]{1,0:T(8,128)(2,1)} %param.9) | copy-start | bytes 1572868
  7.2 94.7 %all-gather.2.cloned.1.call-start = ((), (), s32[]{:S(2)}) async-start(), calls=%async_computation.3 | async-start | bytes 4718592 | tf_op jit(solution)/shard_map/all_gather | solution.py:150
  7.9 281.0 %reduce-scatter.5.cloned.1.call-start = ((), (), s32[]{:S(2)}) async-start(), calls=%async_computation.4 | async-start | bytes 17825792 | tf_op jit(solution)/shard_map/reduce_scatter | solution.py:162
  9.5 7.8 %copy-start.21 = (f32[16,256]{1,0:T(8,128)}, f32[16,256]{1,0:T(8,128)S(1)}, u32[]{:S(2)}) copy-start(f32[16,256]{1,0:T(8,128)S(1)} %copy_bitcast_fusion) | copy-start | bytes 49156
  9.7 5.9 %collective-permute-start.7 = (f32[1,16]{1,0:T(1,128)S(1)}, f32[1,16]{1,0:T(1,128)S(1)}, u32[]{:S(2)}, u32[]{:S(2)}) collective-permute-start(f32[1,16]{1,0:T(1,128)S(1)} %slice_exponential_fusion), channel_id=1, source_target_pairs={{8,0},{16,8},{24,16},{32,24},{40,32},{48,40},{56,48},{64,56},{72,6... | collective-permute-start | bytes 200 | tf_op jit(solution)/shard_map/ppermute | solution.py:33
  11.0 5.8 %collective-permute-start = (f32[1,16]{1,0:T(1,128)S(1)}, f32[1,16]{1,0:T(1,128)S(1)}, u32[]{:S(2)}, u32[]{:S(2)}) collective-permute-start(f32[1,16]{1,0:T(1,128)S(1)} %slice_exponential_fusion), channel_id=1, source_target_pairs={{0,8},{8,16},{16,24},{24,32},{32,40},{40,48},{48,56},{56,64},{64,7... | collective-permute-start | bytes 200 | tf_op jit(solution)/shard_map/ppermute | solution.py:33
  18.1 3.9 %copy-start.9 = (f32[256,16]{1,0:T(8,128)}, f32[256,16]{1,0:T(8,128)S(1)}, u32[]{:S(2)}) copy-start(f32[256,16]{1,0:T(8,128)S(1)} %get-tuple-element.392) | copy-start | bytes 49156
  18.1 3.8 %copy-start.19 = (f32[256,16]{0,1:T(8,128)}, f32[256,16]{0,1:T(8,128)S(1)}, u32[]{:S(2)}) copy-start(f32[256,16]{0,1:T(8,128)S(1)} %copy.100) | copy-start | bytes 49156
  21.3 33.9 %copy-start.1 = (f32[256,1024]{0,1:T(8,128)}, f32[256,1024]{0,1:T(8,128)S(1)}, u32[]{:S(2)}) copy-start(f32[256,1024]{0,1:T(8,128)S(1)} %copy.102) | copy-start | bytes 3145732
  21.9 47.5 %copy-start.29 = (f32[16]{0:T(128)S(1)}, f32[16]{0:T(128)}, u32[]{:S(2)}) copy-start(f32[16]{0:T(128)} %param.14) | copy-start | bytes 196
  22.0 13.8 %collective-permute-start.3 = (bf16[1,16,64,256]{3,2,1,0:T(8,128)(2,1)S(1)}, bf16[1,16,64,256]{3,2,1,0:T(8,128)(2,1)S(1)}, u32[]{:S(2)}, u32[]{:S(2)}) collective-permute-start(bf16[1,16,64,256]{3,2,1,0:T(8,128)(2,1)S(1)} %convert_bitcast_fusion.2), channel_id=1, source_target_pairs={{0,8},{8,16},{16,24},{24,32},{32,40},{40,48},{48,56},{56,64},{64,7... | collective-permute-start | bytes 1572872 | tf_op jit(solution)/shard_map/ppermute | solution.py:34
  26.3 49.9 %copy-start.26 = (f32[16]{0:T(128)}, f32[16]{0:T(128)S(1)}, u32[]{:S(2)}) copy-start(f32[16]{0:T(128)S(1)} %fusion.67) | copy-start | bytes 196
  26.3 56.5 %copy-start.8 = (bf16[256,256]{1,0:T(8,128)(2,1)S(1)}, bf16[256,256]{1,0:T(8,128)(2,1)}, u32[]{:S(2)}) copy-start(bf16[256,256]{1,0:T(8,128)(2,1)} %param.12) | copy-start | bytes 393220
  36.8 16.2 %collective-permute-start.4 = (bf16[1,16,64,256]{3,2,1,0:T(8,128)(2,1)}, bf16[1,16,64,256]{3,2,1,0:T(8,128)(2,1)}, u32[]{:S(2)}, u32[]{:S(2)}) collective-permute-start(bf16[1,16,64,256]{3,2,1,0:T(8,128)(2,1)} %fusion.73), channel_id=1, source_target_pairs={{0,16},{8,24},{16,32},{24,40},{32,48},{40,56},{48,64},{56,72},{64,... | collective-permute-start | bytes 1572872 | tf_op jit(solution)/shard_map/ppermute | solution.py:34
  55.2 19.4 %collective-permute-start.5 = (bf16[1,16,64,256]{3,2,1,0:T(8,128)(2,1)}, bf16[1,16,64,256]{3,2,1,0:T(8,128)(2,1)}, u32[]{:S(2)}, u32[]{:S(2)}) collective-permute-start(bf16[1,16,64,256]{3,2,1,0:T(8,128)(2,1)} %fusion.46), channel_id=1, source_target_pairs={{0,32},{8,40},{16,48},{24,56},{32,64},{40,72},{48,80},{56,88},{64,... | collective-permute-start | bytes 1572872 | tf_op jit(solution)/shard_map/ppermute | solution.py:34
  67.0 19.7 %copy-start.15 = (f32[256,16]{1,0:T(8,128)S(1)}, f32[256,16]{1,0:T(8,128)}, u32[]{:S(2)}) copy-start(f32[256,16]{1,0:T(8,128)} %get-tuple-element.391) | copy-start | bytes 49156
  68.0 2.8 collective-permute-start.1
  76.2 13.8 %collective-permute-start.6 = (bf16[1,16,64,256]{3,2,1,0:T(8,128)(2,1)S(1)}, bf16[1,16,64,256]{3,2,1,0:T(8,128)(2,1)S(1)}, u32[]{:S(2)}, u32[]{:S(2)}) collective-permute-start(bf16[1,16,64,256]{3,2,1,0:T(8,128)(2,1)S(1)} %add_convert_fusion.2), channel_id=1, source_target_pairs={{0,64},{8,72},{16,80},{24,88},{32,96},{40,104},{48,112},{56,120},{... | collective-permute-start | bytes 1572872 | tf_op jit(solution)/shard_map/ppermute | solution.py:34
  83.8 5.6 %collective-permute-start.2 = (f32[1,16]{1,0:T(1,128)S(1)}, f32[1,16]{1,0:T(1,128)S(1)}, u32[]{:S(2)}, u32[]{:S(2)}) collective-permute-start(f32[1,16]{1,0:T(1,128)S(1)} %fusion.62), channel_id=1, source_target_pairs={{0,32},{8,40},{16,48},{24,56},{32,64},{40,72},{48,80},{56,88},{64,... | collective-permute-start | bytes 200 | tf_op jit(solution)/shard_map/ppermute | solution.py:33
  86.8 6.5 %copy-start.17 = (f32[256,256]{1,0:T(8,128)S(1)}, f32[256,256]{1,0:T(8,128)}, u32[]{:S(2)}) copy-start(f32[256,256]{1,0:T(8,128)} %fusion.78) | copy-start | bytes 786436
  86.8 6.5 %copy-start.23 = (pred[256,256]{1,0:T(8,128)(4,1)S(1)}, pred[256,256]{1,0:T(8,128)(4,1)}, u32[]{:S(2)}) copy-start(pred[256,256]{1,0:T(8,128)(4,1)} %iota_compare_fusion) | copy-start | bytes 196612
  90.0 0.8 copy-start.16
  93.3 6.1 %copy-start.6 = (f32[256,1,16,64]{0,3,2,1:T(8,128)}, f32[256,1,16,64]{0,3,2,1:T(8,128)S(1)}, u32[]{:S(2)}) copy-start(f32[256,1,16,64]{0,3,2,1:T(8,128)S(1)} %convolution_bitcast_fusion.1) | copy-start | bytes 3145732
  93.3 8.6 %copy-start.12 = (bf16[256,1024]{1,0:T(8,128)(2,1)S(1)}, bf16[256,1024]{1,0:T(8,128)(2,1)}, u32[]{:S(2)}) copy-start(bf16[256,1024]{1,0:T(8,128)(2,1)} %param.10) | copy-start | bytes 1572868
  114.9 11.4 %copy-start.5 = (f32[256,1024]{1,0:T(8,128)}, f32[256,1024]{1,0:T(8,128)S(1)}, u32[]{:S(2)}) copy-start(f32[256,1024]{1,0:T(8,128)S(1)} %get-tuple-element.381) | copy-start | bytes 3145732
  125.9 185.8 %reduce-scatter.3.cloned.1.call-start = ((), (), s32[]{:S(2)}) async-start(), calls=%async_computation.2 | async-start | bytes 4718592 | tf_op jit(solution)/shard_map/reduce_scatter | solution.py:147
  146.7 33.8 %collective-permute-start.10 = (bf16[1,16,64,256]{3,2,1,0:T(8,128)(2,1)}, bf16[1,16,64,256]{3,2,1,0:T(8,128)(2,1)}, u32[]{:S(2)}, u32[]{:S(2)}) collective-permute-start(bf16[1,16,64,256]{3,2,1,0:T(8,128)(2,1)} %convert_bitcast_fusion.1), channel_id=1, source_target_pairs={{8,0},{16,8},{24,16},{32,24},{40,32},{48,40},{56,48},{64,56},{72,6... | collective-permute-start | bytes 1572872 | tf_op jit(solution)/shard_map/ppermute | solution.py:34
  150.2 7.1 %collective-permute-start.8 = (f32[1,16]{1,0:T(1,128)}, f32[1,16]{1,0:T(1,128)}, u32[]{:S(2)}, u32[]{:S(2)}) collective-permute-start(f32[1,16]{1,0:T(1,128)} %get-tuple-element.377), channel_id=1, source_target_pairs={{16,0},{24,8},{32,16},{40,24},{48,32},{56,40},{64,48},{72,56},{80,... | collective-permute-start | bytes 200 | tf_op jit(solution)/shard_map/ppermute | solution.py:33
  158.5 19.4 %collective-permute-start.9 = (f32[1,16]{1,0:T(1,128)}, f32[1,16]{1,0:T(1,128)}, u32[]{:S(2)}, u32[]{:S(2)}) collective-permute-start(f32[1,16]{1,0:T(1,128)} %fusion.64), channel_id=1, source_target_pairs={{32,0},{40,8},{48,16},{56,24},{64,32},{72,40},{80,48},{88,56},{96,... | collective-permute-start | bytes 200 | tf_op jit(solution)/shard_map/ppermute | solution.py:33
  182.5 28.8 %collective-permute-start.11 = (bf16[1,16,64,256]{3,2,1,0:T(8,128)(2,1)}, bf16[1,16,64,256]{3,2,1,0:T(8,128)(2,1)}, u32[]{:S(2)}, u32[]{:S(2)}) collective-permute-start(bf16[1,16,64,256]{3,2,1,0:T(8,128)(2,1)} %fusion.74), channel_id=1, source_target_pairs={{16,0},{24,8},{32,16},{40,24},{48,32},{56,40},{64,48},{72,56},{80,... | collective-permute-start | bytes 1572872 | tf_op jit(solution)/shard_map/ppermute | solution.py:34
  187.6 26.6 %copy-start.3 = (f32[256,1024]{0,1:T(8,128)S(1)}, f32[256,1024]{0,1:T(8,128)}, u32[]{:S(2)}) copy-start(f32[256,1024]{0,1:T(8,128)} %copy.108) | copy-start | bytes 3145732
  187.6 26.6 %copy-start.14 = (bf16[256,1024]{0,1:T(8,128)(2,1)S(1)}, bf16[256,1024]{0,1:T(8,128)(2,1)}, u32[]{:S(2)}) copy-start(bf16[256,1024]{0,1:T(8,128)(2,1)} %copy.97) | copy-start | bytes 1572868
  187.6 26.6 %copy-start.18 = (f32[256,256]{1,0:T(8,128)S(1)}, f32[256,256]{1,0:T(8,128)}, u32[]{:S(2)}) copy-start(f32[256,256]{1,0:T(8,128)} %fusion.78) | copy-start | bytes 786436
  187.6 26.6 %copy-start.22 = (f32[16,256]{1,0:T(8,128)S(1)}, f32[16,256]{1,0:T(8,128)}, u32[]{:S(2)}) copy-start(f32[16,256]{1,0:T(8,128)} %copy-done.21) | copy-start | bytes 49156
  187.6 26.6 %copy-start.24 = (pred[256,256]{1,0:T(8,128)(4,1)S(1)}, pred[256,256]{1,0:T(8,128)(4,1)}, u32[]{:S(2)}) copy-start(pred[256,256]{1,0:T(8,128)(4,1)} %iota_compare_fusion) | copy-start | bytes 196612
  212.9 25.3 %collective-permute-start.12 = (bf16[1,16,64,256]{3,2,1,0:T(8,128)(2,1)S(1)}, bf16[1,16,64,256]{3,2,1,0:T(8,128)(2,1)S(1)}, u32[]{:S(2)}, u32[]{:S(2)}) collective-permute-start(bf16[1,16,64,256]{3,2,1,0:T(8,128)(2,1)S(1)} %fusion.47), channel_id=1, source_target_pairs={{32,0},{40,8},{48,16},{56,24},{64,32},{72,40},{80,48},{88,56},{96,... | collective-permute-start | bytes 1572872 | tf_op jit(solution)/shard_map/ppermute | solution.py:34
  214.3 23.9 %copy-start.27 = (f32[16]{0:T(128)S(1)}, f32[16]{0:T(128)}, u32[]{:S(2)}) copy-start(f32[16]{0:T(128)} %copy-done.26) | copy-start | bytes 196
  214.3 23.9 %copy-start.28 = (f32[1,16]{1,0:T(1,128)S(1)}, f32[1,16]{1,0:T(1,128)}, u32[]{:S(2)}) copy-start(f32[1,16]{1,0:T(1,128)} %get-tuple-element.377) | copy-start | bytes 196
  219.3 24.1 %copy-start.11 = (f32[256,256]{1,0:T(8,128)}, f32[256,256]{1,0:T(8,128)S(1)}, u32[]{:S(2)}) copy-start(f32[256,256]{1,0:T(8,128)S(1)} %get-tuple-element.372) | copy-start | bytes 786436
  238.2 2.7 copy-start.7
  240.9 19.8 %collective-permute-start.13 = (bf16[1,16,64,256]{3,2,1,0:T(8,128)(2,1)}, bf16[1,16,64,256]{3,2,1,0:T(8,128)(2,1)S(1)}, u32[]{:S(2)}, u32[]{:S(2)}) collective-permute-start(bf16[1,16,64,256]{3,2,1,0:T(8,128)(2,1)} %add_convert_fusion.1), channel_id=1, source_target_pairs={{64,0},{72,8},{80,16},{88,24},{96,32},{104,40},{112,48},{120,56},{... | collective-permute-start | bytes 1572872 | tf_op jit(solution)/shard_map/ppermute | solution.py:34
  245.0 22.9 %copy-start.20 = (f32[256,16]{0,1:T(8,128)S(1)}, f32[256,16]{0,1:T(8,128)}, u32[]{:S(2)}) copy-start(f32[256,16]{0,1:T(8,128)} %copy-done.19) | copy-start | bytes 49156
  260.6 0.8 copy-start.13
  267.9 9.0 %copy-start.10 = (f32[256,16]{1,0:T(8,128)S(1)}, f32[256,16]{1,0:T(8,128)}, u32[]{:S(2)}) copy-start(f32[256,16]{1,0:T(8,128)} %copy-done.9) | copy-start | bytes 49156
  267.9 14.5 %copy-start.2 = (f32[256,1024]{0,1:T(8,128)S(1)}, f32[256,1024]{0,1:T(8,128)}, u32[]{:S(2)}) copy-start(f32[256,1024]{0,1:T(8,128)} %copy-done.1) | copy-start | bytes 3145732
  274.4 12.2 %copy-start.25 = (f32[1024]{0:T(1024)S(1)}, f32[1024]{0:T(1024)}, u32[]{:S(2)}) copy-start(f32[1024]{0:T(1024)} %mul.570) | copy-start | bytes 12292
Sparse Core Ops, SparseCore 0:
  9.7 34.7 all-gather.1
  126.1 145.8 reduce-scatter.4
  274.9 36.7 reduce-scatter.2

commit v2 on v1

--- a/solution.py
+++ b/solution.py
@@ -159,14 +159,19 @@
     decay_after, end_grad = log_scan((own_decay, state_direct), "seq", True)
     input_part, write_grad, read_grad, decay_grad, start_grad = ssd_pull((ssd_grad, end_grad))
     input_grad = skip_input_grad + input_part
-    weight_grad = lax.psum_scatter(
-        jnp.einsum("td,th->dh", full_grad, normed_half, preferred_element_type=jnp.float32).astype(
-            jnp.bfloat16
-        ),
+    seq_count = lax.axis_size("seq")
+    feature_count = full_grad.shape[1]
+    grad_columns = lax.all_to_all(
+        full_grad.reshape(row_count, seq_count, feature_count // seq_count),
         "seq",
-        scatter_dimension=0,
+        split_axis=1,
+        concat_axis=0,
         tiled=True,
-    )
+    ).reshape(seq_count * row_count, feature_count // seq_count)
+    all_normed = lax.all_gather(normed_half, "seq", axis=0, tiled=True)
+    weight_grad = jnp.einsum(
+        "td,th->dh", grad_columns, all_normed, preferred_element_type=jnp.float32
+    ).astype(jnp.bfloat16)
     return (
         layer_out,
         input_grad.astype(jnp.bfloat16),

time: 320 us -> 329 us (1.028)
  starting transfers between devices: 48.1 us -> 59.2 us
  other arithmetic: 41.1 us -> 33.8 us
  waiting for transfers between devices: 122 us -> 129 us
  matrix products: 67.1 us -> 60.2 us
  local copies, waits for them, and re-layouts: 25.5 us -> 31.5 us
    ppermute x8, waiting for transfers between devices: 72.7 us -> 110 us  [log_scan(): lax.ppermute(incl[1].astype(jnp.bfloat16), axis, pairs).astype(jnp.float32)]
    reduce_scatter x1, waiting for transfers between devices: 20.6 us -> 0.01 us  [per_device(): lax.psum_scatter(partial_out.astype(jnp.bfloat16), 'head', scatter_dimens...]
    all_to_all x0 -> x1, starting transfers between devices: none -> 10.7 us  [per_device(): lax.all_to_all(full_grad.reshape(row_count, seq_count, feature_count // s...]
    ppermute x6, waiting for transfers between devices: 28.2 us -> 18.6 us  [log_scan(): got_decay = lax.ppermute(incl[0], axis, pairs)]
    all_to_all x0 -> x1, local copies, waits for them, and re-layouts: none -> 6.29 us  [per_device(): lax.all_to_all(full_grad.reshape(row_count, seq_count, feature_count // s...]
    unnamed x63 -> x80, local copies, waits for them, and re-layouts: 5.73 us -> 8.37 us
  transfers between devices with their start and end apart: 17 -> 18, of which waited for: 12 -> 11; matrix products, arithmetic and copies ran while one was open for 34% -> 33% of each run, Pallas kernels for 0% -> 0%
where the time goes in v2:
time: 329 us; the launch traced here: 328 us
  waiting for transfers between devices  129 us (39%)
  matrix products  60.2 us (18%)
  starting transfers between devices  59.2 us (18%)
  other arithmetic  33.8 us (10%)
  local copies, waits for them, and re-layouts  31.5 us (10%)
  between operations  14.4 us (4%)
    ppermute x8, waiting for transfers between devices, log_scan(): lax.ppermute(incl[1].astype(jnp.bfloat16), axis, pairs).astype(jnp.float32)  110 us
    ppermute x8, starting transfers between devices, log_scan(): lax.ppermute(incl[1].astype(jnp.bfloat16), axis, pairs).astype(jnp.float32)  35.6 us
    ppermute x6, waiting for transfers between devices, log_scan(): got_decay = lax.ppermute(incl[0], axis, pairs)  18.6 us
    dot_general x3, matrix products, block_scan(): jnp.einsum('gkts,sgkp->tgkp', weights, input_heads, precision=highest)  15.8 us
    ppermute x6, starting transfers between devices, log_scan(): got_decay = lax.ppermute(incl[0], axis, pairs)  12.7 us
    convert_element_type x8, other arithmetic, log_scan(): incl[1].astype(jnp.bfloat16)  12.1 us
    all_to_all x1, starting transfers between devices, per_device(): lax.all_to_all(full_grad.reshape(row_count, seq_count, feature_count // s...  10.7 us
    dot_general x1, matrix products, per_device(): jnp.dot(full_grad, out_weight, preferred_element_type=jnp.float32)  10 us
  transfers between devices with their start and end apart: 18, of which 11 were waited for; matrix products, arithmetic and copies ran while one was open for 33% of the time, Pallas kernels for 0%

profile of v2, /device:TPU:0, one launch (start us, length us, event | category | flops | bytes accessed | tf_op | source)
XLA Modules:
  0.0 327.7 jit_solution(561847673965869911)
XLA Ops:
  7.2 2.1 copy.108
  11.1 1.3 collective-permute-start.7
  12.4 4.5 %collective-permute-start = (f32[1,16]{1,0:T(1,128)S(1)}, f32[1,16]{1,0:T(1,128)S(1)}, u32[]{:S(2)}, u32[]{:S(2)}) collective-permute-start(f32[1,16]{1,0:T(1,128)S(1)} %slice_exponential_fusion), channel_id=1, source_target_pairs={{0,8},{8,16},{16,24},{24,32},{32,40},{40,48},{48,56},{56,64},{64,7... | collective-permute-start | bytes 200 | tf_op jit(solution)/shard_map/ppermute | solution.py:33
  17.0 1.3 collective-permute-done
  20.0 1.1 convert_multiply_fusion.2
  21.1 1.6 copy.106
  23.5 4.2 %collective-permute-start.3 = (bf16[1,16,64,256]{3,2,1,0:T(8,128)(2,1)S(1)}, bf16[1,16,64,256]{3,2,1,0:T(8,128)(2,1)S(1)}, u32[]{:S(2)}, u32[]{:S(2)}) collective-permute-start(bf16[1,16,64,256]{3,2,1,0:T(8,128)(2,1)S(1)} %convert_bitcast_fusion.1), channel_id=1, source_target_pairs={{0,8},{8,16},{16,24},{24,32},{32,40},{40,48},{48,56},{56,64},{64,7... | collective-permute-start | bytes 1572872 | tf_op jit(solution)/shard_map/ppermute | solution.py:34
  27.8 9.5 %collective-permute-done.3 = bf16[1,16,64,256]{3,2,1,0:T(8,128)(2,1)S(1)} collective-permute-done((bf16[1,16,64,256]{3,2,1,0:T(8,128)(2,1)S(1)}, bf16[1,16,64,256]{3,2,1,0:T(8,128)(2,1)S(1)}, u32[]{:S(2)}, u32[]{:S(2)}) %collective-permute-start.3) | collective-permute-done | bytes 524320 | tf_op jit(solution)/shard_map/ppermute | solution.py:34
  38.3 7.5 %collective-permute-start.4 = (bf16[1,16,64,256]{3,2,1,0:T(8,128)(2,1)}, bf16[1,16,64,256]{3,2,1,0:T(8,128)(2,1)}, u32[]{:S(2)}, u32[]{:S(2)}) collective-permute-start(bf16[1,16,64,256]{3,2,1,0:T(8,128)(2,1)} %fusion.74), channel_id=1, source_target_pairs={{0,16},{8,24},{16,32},{24,40},{32,48},{40,56},{48,64},{56,72},{64,... | collective-permute-start | bytes 1572872 | tf_op jit(solution)/shard_map/ppermute | solution.py:34
  45.8 8.7 %collective-permute-done.4 = bf16[1,16,64,256]{3,2,1,0:T(8,128)(2,1)} collective-permute-done((bf16[1,16,64,256]{3,2,1,0:T(8,128)(2,1)}, bf16[1,16,64,256]{3,2,1,0:T(8,128)(2,1)}, u32[]{:S(2)}, u32[]{:S(2)}) %collective-permute-start.4) | collective-permute-done | bytes 524320 | tf_op jit(solution)/shard_map/ppermute | solution.py:34
  54.6 2.2 fusion.47
  56.7 11.7 %collective-permute-start.5 = (bf16[1,16,64,256]{3,2,1,0:T(8,128)(2,1)}, bf16[1,16,64,256]{3,2,1,0:T(8,128)(2,1)}, u32[]{:S(2)}, u32[]{:S(2)}) collective-permute-start(bf16[1,16,64,256]{3,2,1,0:T(8,128)(2,1)} %fusion.47), channel_id=1, source_target_pairs={{0,32},{8,40},{16,48},{24,56},{32,64},{40,72},{48,80},{56,88},{64,... | collective-permute-start | bytes 1572872 | tf_op jit(solution)/shard_map/ppermute | solution.py:34
  68.5 1.0 copy.101
  69.5 1.5 collective-permute-start.1
  72.2 3.8 %collective-permute-done.5 = bf16[1,16,64,256]{3,2,1,0:T(8,128)(2,1)} collective-permute-done((bf16[1,16,64,256]{3,2,1,0:T(8,128)(2,1)}, bf16[1,16,64,256]{3,2,1,0:T(8,128)(2,1)}, u32[]{:S(2)}, u32[]{:S(2)}) %collective-permute-start.5) | collective-permute-done | bytes 524320 | tf_op jit(solution)/shard_map/ppermute | solution.py:34
  76.0 1.7 add_convert_fusion.2
  77.7 6.7 %collective-permute-start.6 = (bf16[1,16,64,256]{3,2,1,0:T(8,128)(2,1)S(1)}, bf16[1,16,64,256]{3,2,1,0:T(8,128)(2,1)}, u32[]{:S(2)}, u32[]{:S(2)}) collective-permute-start(bf16[1,16,64,256]{3,2,1,0:T(8,128)(2,1)S(1)} %add_convert_fusion.2), channel_id=1, source_target_pairs={{0,64},{8,72},{16,80},{24,88},{32,96},{40,104},{48,112},{56,120},{... | collective-permute-start | bytes 1572872 | tf_op jit(solution)/shard_map/ppermute | solution.py:34
  86.1 2.8 collective-permute-start.2
  88.9 1.3 copy.110
  90.8 1.9 add_add_fusion.2
  93.4 6.2 %fusion.25 = f32[256,1,16,64]{0,3,2,1:T(8,128)} fusion(bf16[256,16,64]{0,2,1:T(8,128)(2,1)} %bitcast.212, f32[16,256]{1,0:T(8,128)} %copy-done.23, f32[256,256]{1,0:T(8,128)} %fusion.79, pred[256,256]{1,0:T(8,128)(4,1)} %iota_compare_fusion, f32[256,1,16,64]{0,3,2,1:T(8,128)S(1)} %convolution_bitcast_fusion.1, f32[256,16]{0,1:T(8,128)S(1)} %copy.103), kind=kOutput, calls=%fused_computation.33 | convolution fusion | flops 810024960 | bytes 2981888 | tf_op jit(solution)/shard_map/jvp()/while/body/eval_jaxpr/gkts,sgkp->tgkp/dot_general | solution.py:60
  99.5 1.6 copy.107
  101.2 10.0 %multiply_reduce_fusion.4 = (f32[256]{0:T(256)S(1)}, f32[256]{0:T(256)S(1)}, f32[256,1024]{1,0:T(8,128)S(1)}, f32[256,1024]{1,0:T(8,128)S(1)}) fusion(bf16[256,1024]{1,0:T(8,128)(2,1)S(1)} %copy-done.8, f32[256,1024]{1,0:T(8,128)S(1)} %copy.107, f32[1024]{0:T(1024)} %mul.570, bf16[256,1024]{1,0:T(8,128)(2,1)S(1)} %copy-done.1, f32[1024]{0:T(1024)} %param.15, ...), kind=kOutput, calls=%fused_computation.67 | convolution fusion | flops 4298637312 | bytes 25176064 | tf_op jit(solution)/shard_map/dot_general | solution.py:151
  111.2 2.2 fusion.76
  113.7 9.7 %convolution_convert_fusion = bf16[256,8192]{1,0:T(8,128)(2,1)} fusion(bf16[256,1024]{1,0:T(8,128)(2,1)} %get-tuple-element.385, bf16[8192,1024]{1,0:T(8,128)(2,1)} %param.16), kind=kOutput, calls=%fused_computation | convolution fusion | flops 4297064448 | bytes 21495808 | tf_op jit(solution)/shard_map/th,dh->td/dot_general | solution.py:144
  123.4 1.3 copy-done.7
  124.7 1.3 copy.111
  126.0 1.8 fusion.52
  128.7 1.3 collective-permute-start.10
  130.0 1.2 copy.116
  131.1 1.3 collective-permute-start.8
  132.4 5.7 %collective-permute-done.8 = f32[1,16]{1,0:T(1,128)S(1)} collective-permute-done((f32[1,16]{1,0:T(1,128)S(1)}, f32[1,16]{1,0:T(1,128)S(1)}, u32[]{:S(2)}, u32[]{:S(2)}) %collective-permute-start.8) | collective-permute-done | bytes 96 | tf_op jit(solution)/shard_map/ppermute | solution.py:33
  138.1 1.3 collective-permute-start.9
  139.4 10.6 %collective-permute-done.9 = f32[1,16]{1,0:T(1,128)S(1)} collective-permute-done((f32[1,16]{1,0:T(1,128)S(1)}, f32[1,16]{1,0:T(1,128)S(1)}, u32[]{:S(2)}, u32[]{:S(2)}) %collective-permute-start.9) | collective-permute-done | bytes 96 | tf_op jit(solution)/shard_map/ppermute | solution.py:33
  150.6 1.6 copy.113
  152.1 2.1 fusion.75
  154.2 1.3 collective-permute-start.11
  155.5 2.2 multiply_reduce_fusion.1
  157.7 1.5 copy.119
  159.2 10.7 %all-to-all-start = ((bf16[256,16,512]{0,2,1:T(8,128)(2,1)}), bf16[256,16,512]{0,2,1:T(8,128)(2,1)}, u32[]{:S(2)}, u32[]{:S(2)}) async-start(bf16[256,16,512]{0,2,1:T(8,128)(2,1)} %bitcast.190), calls=%async_computation.1 | async-start | bytes 8388608 | tf_op jit(solution)/shard_map/all_to_all | solution.py:164
  169.9 2.5 convolution_bitcast_fusion.3
  172.4 1.6 fusion.73
  174.0 13.2 %collective-permute-done.11 = bf16[1,16,64,256]{3,2,1,0:T(8,128)(2,1)} collective-permute-done((bf16[1,16,64,256]{3,2,1,0:T(8,128)(2,1)}, bf16[1,16,64,256]{3,2,1,0:T(8,128)(2,1)}, u32[]{:S(2)}, u32[]{:S(2)}) %collective-permute-start.11) | collective-permute-done | bytes 524320 | tf_op jit(solution)/shard_map/ppermute | solution.py:34
  187.2 1.5 fusion.48
  188.7 1.3 collective-permute-start.12
  190.1 5.0 %fusion.7 = (f32[16,256]{1,0:T(8,128)S(1)}, f32[16,256]{1,0:T(8,128)}, f32[256,256]{1,0:T(8,128)S(1)}) fusion(f32[16,256]{1,0:T(8,128)S(1)} %copy-done.24, f32[256,256]{1,0:T(8,128)S(1)} %copy-done.17, pred[256,256]{1,0:T(8,128)(4,1)S(1)} %copy-done.26, f32[16,64,256]{2,1,0:T(8,128)S(1)} %bitcast.195, bf16[256,16,64]{0,2,1:T(8,128)(2,1)S(1)} %bitcast.213), kind=kOutput, calls=%fused_computation.9 | convolution fusion | flops 816766976 | bytes 2211840 | tf_op jit(solution)/shard_map/transpose(jvp())/while/body/eval_jaxpr/gkts,sgkp->tgkp/dot_general | solution.py:60
  195.1 64.8 %collective-permute-done.12 = bf16[1,16,64,256]{3,2,1,0:T(8,128)(2,1)S(1)} collective-permute-done((bf16[1,16,64,256]{3,2,1,0:T(8,128)(2,1)S(1)}, bf16[1,16,64,256]{3,2,1,0:T(8,128)(2,1)S(1)}, u32[]{:S(2)}, u32[]{:S(2)}) %collective-permute-start.12) | collective-permute-done | bytes 524320 | tf_op jit(solution)/shard_map/ppermute | solution.py:34
  260.0 2.7 add_convert_fusion.1
  262.7 1.5 collective-permute-start.13
  264.2 1.0 convolution_bitcast_fusion.2
  266.9 2.0 fusion.33
  268.9 9.9 %collective-permute-done.13 = bf16[1,16,64,256]{3,2,1,0:T(8,128)(2,1)S(1)} collective-permute-done((bf16[1,16,64,256]{3,2,1,0:T(8,128)(2,1)}, bf16[1,16,64,256]{3,2,1,0:T(8,128)(2,1)S(1)}, u32[]{:S(2)}, u32[]{:S(2)}) %collective-permute-start.13) | collective-permute-done | bytes 524320 | tf_op jit(solution)/shard_map/ppermute | solution.py:34
  279.7 2.2 multiply_reduce_fusion.2
  281.8 2.5 multiply_reduce_fusion.3
  284.4 4.7 %fusion.28 = f32[256,1,16,64]{0,3,2,1:T(8,128)} fusion(f32[16,64,256]{2,1,0:T(8,128)S(1)} %bitcast.196, f32[16,256]{1,0:T(8,128)S(1)} %copy-done.25, f32[256,256]{1,0:T(8,128)S(1)} %copy-done.18, pred[256,256]{1,0:T(8,128)(4,1)S(1)} %copy-done.27, f32[256,1,16,64]{0,3,2,1:T(8,128)S(1)} %get-tuple-element.402, f32[256,16]{0,1:T(8,128)S(1)} %copy-done.22), kind=kOutput, calls=%fused_computation.34 | convolution fusion | flops 810024960 | bytes 3506176 | tf_op jit(solution)/shard_map/transpose(jvp())/while/body/eval_jaxpr/gkts,sgkp->tgkp/dot_general | solution.py:60
  289.0 2.6 copy.114
  291.7 3.4 %fusion.34 = bf16[256,256]{0,1:T(8,128)(2,1)} fusion(f32[256,1,256]{0,2,1:T(8,128)} %convolution_bitcast_fusion.2, f32[256,16,64]{0,2,1:T(8,128)S(1)} %bitcast.192, f32[1,16,64,256]{3,2,1,0:T(8,128)S(1)} %get-tuple-element.376), kind=kOutput, calls=%fused_computation.42 | convolution fusion | flops 805437440 | bytes 2490368 | tf_op jit(solution)/shard_map/transpose(jvp())/while/body/eval_jaxpr/sgkp,sgn->gkpn/dot_general | solution.py:65
  295.1 1.7 copy.125
  297.7 1.2 add_add_fusion.3
  298.9 2.5 reduce-window.36
  302.2 2.2 add_convert_fusion
  304.4 6.3 %copy.124 = bf16[16,256,1,512]{3,1,0,2:T(8,128)(2,1)} copy(bf16[16,256,1,512]{1,3,0,2:T(8,128)(2,1)} %bitcast.68) | data formatting | bytes 8388608 | tf_op jit(solution)/shard_map/all_to_all | solution.py:164
  310.7 9.1 %fusion.21 = bf16[512,1024]{0,1:T(8,128)(2,1)S(1)} fusion(bf16[4096,1024]{1,0:T(8,128)(2,1)} %all-gather.5.cloned.1.call-done, bf16[4096,512]{1,0:T(8,128)(2,1)} %bitcast.198), kind=kOutput, calls=%fused_computation.28 | convolution fusion | flops 4295491584 | bytes 13631488 | tf_op jit(solution)/shard_map/td,th->dh/dot_general | solution.py:172
  319.8 1.3 copy.126
  (131 shorter events, 15.5 us)
Async XLA Ops:
  7.2 15.6 %copy-start = (bf16[256,256]{1,0:T(8,128)(2,1)S(1)}, bf16[256,256]{1,0:T(8,128)(2,1)}, u32[]{:S(2)}) copy-start(bf16[256,256]{1,0:T(8,128)(2,1)} %param.11) | copy-start | bytes 393220
  7.2 12.8 %copy-start.1 = (bf16[256,1024]{1,0:T(8,128)(2,1)S(1)}, bf16[256,1024]{1,0:T(8,128)(2,1)}, u32[]{:S(2)}) copy-start(bf16[256,1024]{1,0:T(8,128)(2,1)} %param.9) | copy-start | bytes 1572868
  7.2 93.9 %all-gather.3.cloned.1.call-start = ((), (), s32[]{:S(2)}) async-start(), calls=%async_computation.3 | async-start | bytes 4718592 | tf_op jit(solution)/shard_map/all_gather | solution.py:150
  9.4 301.3 %all-gather.5.cloned.1.call-start = ((), (), s32[]{:S(2)}) async-start(), calls=%async_computation.4 | async-start | bytes 8912896 | tf_op jit(solution)/shard_map/all_gather | solution.py:171
  11.0 7.8 %copy-start.23 = (f32[16,256]{1,0:T(8,128)}, f32[16,256]{1,0:T(8,128)S(1)}, u32[]{:S(2)}) copy-start(f32[16,256]{1,0:T(8,128)S(1)} %copy_bitcast_fusion) | copy-start | bytes 49156
  11.1 5.9 %collective-permute-start.7 = (f32[1,16]{1,0:T(1,128)S(1)}, f32[1,16]{1,0:T(1,128)S(1)}, u32[]{:S(2)}, u32[]{:S(2)}) collective-permute-start(f32[1,16]{1,0:T(1,128)S(1)} %slice_exponential_fusion), channel_id=1, source_target_pairs={{8,0},{16,8},{24,16},{32,24},{40,32},{48,40},{56,48},{64,56},{72,6... | collective-permute-start | bytes 200 | tf_op jit(solution)/shard_map/ppermute | solution.py:33
  12.4 5.8 %collective-permute-start = (f32[1,16]{1,0:T(1,128)S(1)}, f32[1,16]{1,0:T(1,128)S(1)}, u32[]{:S(2)}, u32[]{:S(2)}) collective-permute-start(f32[1,16]{1,0:T(1,128)S(1)} %slice_exponential_fusion), channel_id=1, source_target_pairs={{0,8},{8,16},{16,24},{24,32},{32,40},{40,48},{48,56},{56,64},{64,7... | collective-permute-start | bytes 200 | tf_op jit(solution)/shard_map/ppermute | solution.py:33
  19.5 3.9 %copy-start.11 = (f32[256,16]{1,0:T(8,128)}, f32[256,16]{1,0:T(8,128)S(1)}, u32[]{:S(2)}) copy-start(f32[256,16]{1,0:T(8,128)S(1)} %get-tuple-element.393) | copy-start | bytes 49156
  19.6 3.8 %copy-start.21 = (f32[256,16]{0,1:T(8,128)}, f32[256,16]{0,1:T(8,128)S(1)}, u32[]{:S(2)}) copy-start(f32[256,16]{0,1:T(8,128)S(1)} %copy.104) | copy-start | bytes 49156
  22.8 34.0 %copy-start.2 = (f32[256,1024]{0,1:T(8,128)}, f32[256,1024]{0,1:T(8,128)S(1)}, u32[]{:S(2)}) copy-start(f32[256,1024]{0,1:T(8,128)S(1)} %copy.106) | copy-start | bytes 3145732
  23.4 47.5 %copy-start.37 = (f32[16]{0:T(128)S(1)}, f32[16]{0:T(128)}, u32[]{:S(2)}) copy-start(f32[16]{0:T(128)} %param.14) | copy-start | bytes 196
  23.5 13.8 %collective-permute-start.3 = (bf16[1,16,64,256]{3,2,1,0:T(8,128)(2,1)S(1)}, bf16[1,16,64,256]{3,2,1,0:T(8,128)(2,1)S(1)}, u32[]{:S(2)}, u32[]{:S(2)}) collective-permute-start(bf16[1,16,64,256]{3,2,1,0:T(8,128)(2,1)S(1)} %convert_bitcast_fusion.1), channel_id=1, source_target_pairs={{0,8},{8,16},{16,24},{24,32},{32,40},{40,48},{48,56},{56,64},{64,7... | collective-permute-start | bytes 1572872 | tf_op jit(solution)/shard_map/ppermute | solution.py:34
  27.8 49.9 %copy-start.28 = (f32[16]{0:T(128)}, f32[16]{0:T(128)S(1)}, u32[]{:S(2)}) copy-start(f32[16]{0:T(128)S(1)} %fusion.68) | copy-start | bytes 196
  27.8 57.3 %copy-start.10 = (bf16[256,256]{1,0:T(8,128)(2,1)S(1)}, bf16[256,256]{1,0:T(8,128)(2,1)}, u32[]{:S(2)}) copy-start(bf16[256,256]{1,0:T(8,128)(2,1)} %param.12) | copy-start | bytes 393220
  38.3 16.3 %collective-permute-start.4 = (bf16[1,16,64,256]{3,2,1,0:T(8,128)(2,1)}, bf16[1,16,64,256]{3,2,1,0:T(8,128)(2,1)}, u32[]{:S(2)}, u32[]{:S(2)}) collective-permute-start(bf16[1,16,64,256]{3,2,1,0:T(8,128)(2,1)} %fusion.74), channel_id=1, source_target_pairs={{0,16},{8,24},{16,32},{24,40},{32,48},{40,56},{48,64},{56,72},{64,... | collective-permute-start | bytes 1572872 | tf_op jit(solution)/shard_map/ppermute | solution.py:34
  56.7 19.3 %collective-permute-start.5 = (bf16[1,16,64,256]{3,2,1,0:T(8,128)(2,1)}, bf16[1,16,64,256]{3,2,1,0:T(8,128)(2,1)}, u32[]{:S(2)}, u32[]{:S(2)}) collective-permute-start(bf16[1,16,64,256]{3,2,1,0:T(8,128)(2,1)} %fusion.47), channel_id=1, source_target_pairs={{0,32},{8,40},{16,48},{24,56},{32,64},{40,72},{48,80},{56,88},{64,... | collective-permute-start | bytes 1572872 | tf_op jit(solution)/shard_map/ppermute | solution.py:34
  68.5 17.5 %copy-start.16 = (f32[256,16]{1,0:T(8,128)S(1)}, f32[256,16]{1,0:T(8,128)}, u32[]{:S(2)}) copy-start(f32[256,16]{1,0:T(8,128)} %get-tuple-element.392) | copy-start | bytes 49156
  68.5 22.3 %copy-start.34 = (f32[1,16]{1,0:T(1,128)S(1)}, f32[1,16]{1,0:T(1,128)}, u32[]{:S(2)}) copy-start(f32[1,16]{1,0:T(1,128)} %get-tuple-element.389) | copy-start | bytes 196
  69.5 2.7 collective-permute-start.1
  77.7 13.1 %collective-permute-start.6 = (bf16[1,16,64,256]{3,2,1,0:T(8,128)(2,1)S(1)}, bf16[1,16,64,256]{3,2,1,0:T(8,128)(2,1)}, u32[]{:S(2)}, u32[]{:S(2)}) collective-permute-start(bf16[1,16,64,256]{3,2,1,0:T(8,128)(2,1)S(1)} %add_convert_fusion.2), channel_id=1, source_target_pairs={{0,64},{8,72},{16,80},{24,88},{32,96},{40,104},{48,112},{56,120},{... | collective-permute-start | bytes 1572872 | tf_op jit(solution)/shard_map/ppermute | solution.py:34
  86.1 4.7 %collective-permute-start.2 = (f32[1,16]{1,0:T(1,128)S(1)}, f32[1,16]{1,0:T(1,128)S(1)}, u32[]{:S(2)}, u32[]{:S(2)}) collective-permute-start(f32[1,16]{1,0:T(1,128)S(1)} %fusion.63), channel_id=1, source_target_pairs={{0,32},{8,40},{16,48},{24,56},{32,64},{40,72},{48,80},{56,88},{64,... | collective-permute-start | bytes 200 | tf_op jit(solution)/shard_map/ppermute | solution.py:33
  93.3 6.2 %copy-start.5 = (f32[256,1,16,64]{0,3,2,1:T(8,128)}, f32[256,1,16,64]{0,3,2,1:T(8,128)S(1)}, u32[]{:S(2)}) copy-start(f32[256,1,16,64]{0,3,2,1:T(8,128)S(1)} %convolution_bitcast_fusion.1) | copy-start | bytes 3145732
  93.3 7.8 %copy-start.8 = (bf16[256,1024]{1,0:T(8,128)(2,1)S(1)}, bf16[256,1024]{1,0:T(8,128)(2,1)}, u32[]{:S(2)}) copy-start(bf16[256,1024]{1,0:T(8,128)(2,1)} %param.10) | copy-start | bytes 1572868
  101.1 10.1 %copy-start.6 = (f32[256,1024]{1,0:T(8,128)S(1)}, f32[256,1024]{1,0:T(8,128)}, u32[]{:S(2)}) copy-start(f32[256,1024]{1,0:T(8,128)} %copy.110) | copy-start | bytes 3145732
  101.2 10.1 %copy-start.19 = (f32[1024]{0:T(1024)S(1)}, f32[1024]{0:T(1024)}, u32[]{:S(2)}) copy-start(f32[1024]{0:T(1024)} %mul.570) | copy-start | bytes 12292
  101.2 10.1 %copy-start.30 = (f32[1024]{0:T(1024)S(1)}, f32[1024]{0:T(1024)}, u32[]{:S(2)}) copy-start(f32[1024]{0:T(1024)} %param.15) | copy-start | bytes 12292
  113.5 207.7 %reduce-scatter.2.cloned.1.call-start = ((), (), s32[]{:S(2)}) async-start(), calls=%async_computation.2 | async-start | bytes 4718592 | tf_op jit(solution)/shard_map/reduce_scatter | solution.py:147
  123.4 1.3 copy-start.7
  123.4 7.7 %copy-start.31 = (f32[1,16]{1,0:T(1,128)S(1)}, f32[1,16]{1,0:T(1,128)}, u32[]{:S(2)}) copy-start(f32[1,16]{1,0:T(1,128)} %get-tuple-element.377) | copy-start | bytes 196
  123.4 26.5 %copy-start.33 = (f32[1,16]{1,0:T(1,128)S(1)}, f32[1,16]{1,0:T(1,128)}, u32[]{:S(2)}) copy-start(f32[1,16]{1,0:T(1,128)} %get-tuple-element.378) | copy-start | bytes 196
  128.7 23.4 %collective-permute-start.10 = (bf16[1,16,64,256]{3,2,1,0:T(8,128)(2,1)}, bf16[1,16,64,256]{3,2,1,0:T(8,128)(2,1)}, u32[]{:S(2)}, u32[]{:S(2)}) collective-permute-start(bf16[1,16,64,256]{3,2,1,0:T(8,128)(2,1)} %convert_bitcast_fusion), channel_id=1, source_target_pairs={{8,0},{16,8},{24,16},{32,24},{40,32},{48,40},{56,48},{64,56},{72,6... | collective-permute-start | bytes 1572872 | tf_op jit(solution)/shard_map/ppermute | solution.py:34
  131.1 7.0 %collective-permute-start.8 = (f32[1,16]{1,0:T(1,128)S(1)}, f32[1,16]{1,0:T(1,128)S(1)}, u32[]{:S(2)}, u32[]{:S(2)}) collective-permute-start(f32[1,16]{1,0:T(1,128)S(1)} %copy-done.31), channel_id=1, source_target_pairs={{16,0},{24,8},{32,16},{40,24},{48,32},{56,40},{64,48},{72,56},{80,... | collective-permute-start | bytes 200 | tf_op jit(solution)/shard_map/ppermute | solution.py:33
  138.1 12.4 %copy-start.35 = (f32[1,16]{1,0:T(1,128)}, f32[1,16]{1,0:T(1,128)S(1)}, u32[]{:S(2)}) copy-start(f32[1,16]{1,0:T(1,128)S(1)} %fusion.65) | copy-start | bytes 196
  138.1 11.8 %collective-permute-start.9 = (f32[1,16]{1,0:T(1,128)S(1)}, f32[1,16]{1,0:T(1,128)S(1)}, u32[]{:S(2)}, u32[]{:S(2)}) collective-permute-start(f32[1,16]{1,0:T(1,128)S(1)} %fusion.65), channel_id=1, source_target_pairs={{32,0},{40,8},{48,16},{56,24},{64,32},{72,40},{80,48},{88,56},{96,... | collective-permute-start | bytes 200 | tf_op jit(solution)/shard_map/ppermute | solution.py:33
  154.2 33.0 %collective-permute-start.11 = (bf16[1,16,64,256]{3,2,1,0:T(8,128)(2,1)}, bf16[1,16,64,256]{3,2,1,0:T(8,128)(2,1)}, u32[]{:S(2)}, u32[]{:S(2)}) collective-permute-start(bf16[1,16,64,256]{3,2,1,0:T(8,128)(2,1)} %fusion.75), channel_id=1, source_target_pairs={{16,0},{24,8},{32,16},{40,24},{48,32},{56,40},{64,48},{72,56},{80,... | collective-permute-start | bytes 1572872 | tf_op jit(solution)/shard_map/ppermute | solution.py:34
  159.2 145.3 %all-to-all-start = ((bf16[256,16,512]{0,2,1:T(8,128)(2,1)}), bf16[256,16,512]{0,2,1:T(8,128)(2,1)}, u32[]{:S(2)}, u32[]{:S(2)}) async-start(bf16[256,16,512]{0,2,1:T(8,128)(2,1)} %bitcast.190), calls=%async_computation.1 | async-start | bytes 8388608 | tf_op jit(solution)/shard_map/all_to_all | solution.py:164
  169.9 20.2 %copy-start.15 = (bf16[256,1024]{0,1:T(8,128)(2,1)S(1)}, bf16[256,1024]{0,1:T(8,128)(2,1)}, u32[]{:S(2)}) copy-start(bf16[256,1024]{0,1:T(8,128)(2,1)} %copy.101) | copy-start | bytes 1572868
  169.9 20.2 %copy-start.17 = (f32[256,256]{1,0:T(8,128)S(1)}, f32[256,256]{1,0:T(8,128)}, u32[]{:S(2)}) copy-start(f32[256,256]{1,0:T(8,128)} %fusion.79) | copy-start | bytes 786436
  169.9 20.2 %copy-start.24 = (f32[16,256]{1,0:T(8,128)S(1)}, f32[16,256]{1,0:T(8,128)}, u32[]{:S(2)}) copy-start(f32[16,256]{1,0:T(8,128)} %copy-done.23) | copy-start | bytes 49156
  169.9 20.2 %copy-start.26 = (pred[256,256]{1,0:T(8,128)(4,1)S(1)}, pred[256,256]{1,0:T(8,128)(4,1)}, u32[]{:S(2)}) copy-start(pred[256,256]{1,0:T(8,128)(4,1)} %iota_compare_fusion) | copy-start | bytes 196612
  188.7 71.2 %collective-permute-start.12 = (bf16[1,16,64,256]{3,2,1,0:T(8,128)(2,1)S(1)}, bf16[1,16,64,256]{3,2,1,0:T(8,128)(2,1)S(1)}, u32[]{:S(2)}, u32[]{:S(2)}) collective-permute-start(bf16[1,16,64,256]{3,2,1,0:T(8,128)(2,1)S(1)} %fusion.48), channel_id=1, source_target_pairs={{32,0},{40,8},{48,16},{56,24},{64,32},{72,40},{80,48},{88,56},{96,... | collective-permute-start | bytes 1572872 | tf_op jit(solution)/shard_map/ppermute | solution.py:34
  190.1 69.9 %copy-start.29 = (f32[16]{0:T(128)S(1)}, f32[16]{0:T(128)}, u32[]{:S(2)}) copy-start(f32[16]{0:T(128)} %copy-done.28) | copy-start | bytes 196
  190.1 69.9 %copy-start.32 = (f32[1,16]{1,0:T(1,128)S(1)}, f32[1,16]{1,0:T(1,128)}, u32[]{:S(2)}) copy-start(f32[1,16]{1,0:T(1,128)} %get-tuple-element.377) | copy-start | bytes 196
  190.1 69.9 %copy-start.36 = (f32[1,16]{1,0:T(1,128)S(1)}, f32[1,16]{1,0:T(1,128)}, u32[]{:S(2)}) copy-start(f32[1,16]{1,0:T(1,128)} %copy-done.35) | copy-start | bytes 196
  195.1 70.1 %copy-start.13 = (f32[256,256]{1,0:T(8,128)}, f32[256,256]{1,0:T(8,128)S(1)}, u32[]{:S(2)}) copy-start(f32[256,256]{1,0:T(8,128)S(1)} %get-tuple-element.372) | copy-start | bytes 786436
  260.0 2.8 copy-start.9
  262.7 16.1 %collective-permute-start.13 = (bf16[1,16,64,256]{3,2,1,0:T(8,128)(2,1)}, bf16[1,16,64,256]{3,2,1,0:T(8,128)(2,1)S(1)}, u32[]{:S(2)}, u32[]{:S(2)}) collective-permute-start(bf16[1,16,64,256]{3,2,1,0:T(8,128)(2,1)} %add_convert_fusion.1), channel_id=1, source_target_pairs={{64,0},{72,8},{80,16},{88,24},{96,32},{104,40},{112,48},{120,56},{... | collective-permute-start | bytes 1572872 | tf_op jit(solution)/shard_map/ppermute | solution.py:34
  266.9 17.5 %copy-start.18 = (f32[256,256]{1,0:T(8,128)S(1)}, f32[256,256]{1,0:T(8,128)}, u32[]{:S(2)}) copy-start(f32[256,256]{1,0:T(8,128)} %fusion.79) | copy-start | bytes 786436
  266.9 17.5 %copy-start.22 = (f32[256,16]{0,1:T(8,128)S(1)}, f32[256,16]{0,1:T(8,128)}, u32[]{:S(2)}) copy-start(f32[256,16]{0,1:T(8,128)} %copy-done.21) | copy-start | bytes 49156
  266.9 17.5 %copy-start.25 = (f32[16,256]{1,0:T(8,128)S(1)}, f32[16,256]{1,0:T(8,128)}, u32[]{:S(2)}) copy-start(f32[16,256]{1,0:T(8,128)} %copy-done.23) | copy-start | bytes 49156
  266.9 17.5 %copy-start.27 = (pred[256,256]{1,0:T(8,128)(4,1)S(1)}, pred[256,256]{1,0:T(8,128)(4,1)}, u32[]{:S(2)}) copy-start(pred[256,256]{1,0:T(8,128)(4,1)} %iota_compare_fusion) | copy-start | bytes 196612
  278.8 0.9 copy-start.14
  284.4 7.3 %copy-start.3 = (f32[256,1024]{0,1:T(8,128)S(1)}, f32[256,1024]{0,1:T(8,128)}, u32[]{:S(2)}) copy-start(f32[256,1024]{0,1:T(8,128)} %copy-done.2) | copy-start | bytes 3145732
  289.0 8.6 %copy-start.12 = (f32[256,16]{1,0:T(8,128)S(1)}, f32[256,16]{1,0:T(8,128)}, u32[]{:S(2)}) copy-start(f32[256,16]{1,0:T(8,128)} %copy-done.11) | copy-start | bytes 49156
  289.0 13.2 %copy-start.4 = (f32[256,1024]{1,0:T(8,128)S(1)}, f32[256,1024]{1,0:T(8,128)}, u32[]{:S(2)}) copy-start(f32[256,1024]{1,0:T(8,128)} %get-tuple-element.380) | copy-start | bytes 3145732
  289.0 13.2 %copy-start.20 = (f32[1024]{0:T(1024)S(1)}, f32[1024]{0:T(1024)}, u32[]{:S(2)}) copy-start(f32[1024]{0:T(1024)} %mul.570) | copy-start | bytes 12292
Sparse Core Ops, SparseCore 0:
  10.3 34.8 all-gather.2
  113.6 136.5 all-gather.4
  253.1 38.5 reduce-scatter.1

commit v3 on v2

--- a/solution.py
+++ b/solution.py
@@ -3,13 +3,14 @@
 import jax
 import jax.numpy as jnp
 from jax import lax
-from jax.sharding import PartitionSpec as P
+from jax.sharding import Mesh, PartitionSpec as P
 
 HALF_HEADS = 128
 P_SIZE = 64
 N = 256
 G = 8
 SPAN = 256
+SEQ = ("sx", "sy")
 
 
 epsilon = 1e-05
@@ -134,7 +135,7 @@
     )
     cumulative = jnp.cumsum(log_decay, axis=0)
     own_decay = jnp.exp(cumulative[-1]).reshape(group_count, per_group)
-    decay_before, start_state = log_scan((own_decay, own_state), "seq", False)
+    decay_before, start_state = log_scan((own_decay, own_state), SEQ, False)
     (ssd_out, end_state), ssd_pull = jax.vjp(
         ssd_run, inputs, writes, reading, log_decay, start_state
     )
@@ -156,22 +157,27 @@
     state_direct = jnp.einsum(
         "tgkp,tgn->gkpn", scaled_grad, reading.reshape(row_count, group_count, N), precision=highest
     )
-    decay_after, end_grad = log_scan((own_decay, state_direct), "seq", True)
+    decay_after, end_grad = log_scan((own_decay, state_direct), SEQ, True)
     input_part, write_grad, read_grad, decay_grad, start_grad = ssd_pull((ssd_grad, end_grad))
     input_grad = skip_input_grad + input_part
-    seq_count = lax.axis_size("seq")
+    rows = lax.axis_size("sx")
+    cols = lax.axis_size("sy")
     feature_count = full_grad.shape[1]
+    block = feature_count // (rows * cols)
     grad_columns = lax.all_to_all(
-        full_grad.reshape(row_count, seq_count, feature_count // seq_count),
-        "seq",
-        split_axis=1,
+        full_grad.reshape(row_count, rows, cols, block),
+        "sy",
+        split_axis=2,
         concat_axis=0,
         tiled=True,
-    ).reshape(seq_count * row_count, feature_count // seq_count)
-    all_normed = lax.all_gather(normed_half, "seq", axis=0, tiled=True)
-    weight_grad = jnp.einsum(
-        "td,th->dh", grad_columns, all_normed, preferred_element_type=jnp.float32
+    ).reshape(cols * row_count, rows, block)
+    row_normed = lax.all_gather(normed_half, "sy", axis=0, tiled=True)
+    row_partial = jnp.einsum(
+        "txd,th->xdh", grad_columns, row_normed, preferred_element_type=jnp.float32
     ).astype(jnp.bfloat16)
+    weight_grad = lax.psum_scatter(row_partial, "sx", scatter_dimension=0, tiled=True).reshape(
+        block, row_normed.shape[1]
+    )
     return (
         layer_out,
         input_grad.astype(jnp.bfloat16),
@@ -185,25 +191,27 @@
 
 def solution(mesh):
     in_specs = (
-        P("seq", "head"),
-        P("seq", "head"),
-        P("seq", "head"),
-        P("seq", "head"),
-        P("seq", "head"),
+        P(SEQ, "head"),
+        P(SEQ, "head"),
+        P(SEQ, "head"),
+        P(SEQ, "head"),
+        P(SEQ, "head"),
         P("head"),
         P("head"),
         P(None, "head"),
-        P("seq", "head"),
+        P(SEQ, "head"),
     )
     out_specs = (
-        P("seq", "head"),
-        P("seq", "head"),
-        P("seq", "head"),
-        P("seq", "head"),
-        P("seq", "head"),
-        P("seq", "head"),
-        P("seq", "head"),
-    )
+        P(SEQ, "head"),
+        P(SEQ, "head"),
+        P(SEQ, "head"),
+        P(SEQ, "head"),
+        P(SEQ, "head"),
+        P(SEQ, "head"),
+        P(SEQ, "head"),
+    )
+    rows = mesh.devices.shape[0] // 4
+    grid = Mesh(mesh.devices.reshape(rows, 4, mesh.devices.shape[1]), ("sx", "sy", "head"))
     return jax.shard_map(
-        per_device, mesh=mesh, in_specs=in_specs, out_specs=out_specs, check_vma=False
-    )
+        per_device, mesh=grid, in_specs=in_specs, out_specs=out_specs, check_vma=False
+    )

time: 329 us -> 319 us (0.970)
  starting transfers between devices: 59.2 us -> 48.8 us
  waiting for transfers between devices: 129 us -> 121 us
  local copies, waits for them, and re-layouts: 31.5 us -> 36.4 us
    ppermute x8, waiting for transfers between devices: 110 us -> 41.9 us  [log_scan(): lax.ppermute(incl[1].astype(jnp.bfloat16), axis, pairs).astype(jnp.float32)]
    all_to_all x1, waiting for transfers between devices: 0.01 us -> 49 us  [per_device(): lax.all_to_all(full_grad.reshape(row_count, rows, cols, block), 'sy', spl...]
    ppermute x6, waiting for transfers between devices: 18.6 us -> 30.1 us  [log_scan(): got_decay = lax.ppermute(incl[0], axis, pairs)]
    reshape x0 -> x1, local copies, waits for them, and re-layouts: none -> 7.32 us  [per_device(): full_grad.reshape(row_count, rows, cols, block)]
    all_to_all x1, starting transfers between devices: 10.7 us -> 5 us  [per_device(): lax.all_to_all(full_grad.reshape(row_count, rows, cols, block), 'sy', spl...]
    ppermute x8, starting transfers between devices: 35.6 us -> 31.5 us  [log_scan(): lax.ppermute(incl[1].astype(jnp.bfloat16), axis, pairs).astype(jnp.float32)]
    unnamed x80 -> x82, local copies, waits for them, and re-layouts: 8.37 us -> 9.27 us
  transfers between devices with their start and end apart: 18 -> 19, of which waited for: 11 -> 12; matrix products, arithmetic and copies ran while one was open for 33% -> 35% of each run, Pallas kernels for 0% -> 0%
where the time goes in v3:
time: 319 us; the launch traced here: 316 us
  waiting for transfers between devices  121 us (38%)
  matrix products  60.8 us (19%)
  starting transfers between devices  48.8 us (15%)
  local copies, waits for them, and re-layouts  36.4 us (11%)
  other arithmetic  34.7 us (11%)
  between operations  14.4 us (5%)
    all_to_all x1, waiting for transfers between devices, per_device(): lax.all_to_all(full_grad.reshape(row_count, rows, cols, block), 'sy', spl...  49 us
    ppermute x8, waiting for transfers between devices, log_scan(): lax.ppermute(incl[1].astype(jnp.bfloat16), axis, pairs).astype(jnp.float32)  41.9 us
    ppermute x8, starting transfers between devices, log_scan(): lax.ppermute(incl[1].astype(jnp.bfloat16), axis, pairs).astype(jnp.float32)  31.5 us
    ppermute x6, waiting for transfers between devices, log_scan(): got_decay = lax.ppermute(incl[0], axis, pairs)  30.1 us
    dot_general x3, matrix products, block_scan(): jnp.einsum('gkts,sgkp->tgkp', weights, input_heads, precision=highest)  16.3 us
    convert_element_type x8, other arithmetic, log_scan(): incl[1].astype(jnp.bfloat16)  12.3 us
    ppermute x6, starting transfers between devices, log_scan(): got_decay = lax.ppermute(incl[0], axis, pairs)  11.9 us
    dot_general x1, matrix products, per_device(): jnp.dot(full_grad, out_weight, preferred_element_type=jnp.float32)  9.95 us
  transfers between devices with their start and end apart: 19, of which 12 were waited for; matrix products, arithmetic and copies ran while one was open for 35% of the time, Pallas kernels for 0%

profile of v3, /device:TPU:0, one launch (start us, length us, event | category | flops | bytes accessed | tf_op | source)
XLA Modules:
  0.0 316.1 jit_solution(11604587841764757727)
XLA Ops:
  7.2 2.1 copy.158
  11.1 3.6 %collective-permute-start = (f32[1,16]{1,0:T(1,128)S(1)}, f32[1,16]{1,0:T(1,128)S(1)}, u32[]{:S(2)}, u32[]{:S(2)}) collective-permute-start(f32[1,16]{1,0:T(1,128)S(1)} %slice_exponential_fusion), channel_id=1, source_target_pairs={{0,8},{8,16},{16,24},{24,32},{32,40},{40,48},{48,56},{56,64},{64,7... | collective-permute-start | bytes 200 | tf_op jit(solution)/shard_map/ppermute | solution.py:34
  14.7 1.3 collective-permute-start.7
  16.0 4.1 %collective-permute-done.7 = f32[1,16]{1,0:T(1,128)S(1)} collective-permute-done((f32[1,16]{1,0:T(1,128)S(1)}, f32[1,16]{1,0:T(1,128)S(1)}, u32[]{:S(2)}, u32[]{:S(2)}) %collective-permute-start.7) | collective-permute-done | bytes 96 | tf_op jit(solution)/shard_map/ppermute | solution.py:34
  21.9 1.1 convert_multiply_fusion.2
  23.0 1.7 copy.156
  25.5 3.5 %collective-permute-start.3 = (bf16[1,16,64,256]{3,2,1,0:T(8,128)(2,1)S(1)}, bf16[1,16,64,256]{3,2,1,0:T(8,128)(2,1)S(1)}, u32[]{:S(2)}, u32[]{:S(2)}) collective-permute-start(bf16[1,16,64,256]{3,2,1,0:T(8,128)(2,1)S(1)} %convert_bitcast_fusion.2), channel_id=1, source_target_pairs={{0,8},{8,16},{16,24},{24,32},{32,40},{40,48},{48,56},{56,64},{64,7... | collective-permute-start | bytes 1572872 | tf_op jit(solution)/shard_map/ppermute | solution.py:35
  29.0 9.6 %collective-permute-done.3 = bf16[1,16,64,256]{3,2,1,0:T(8,128)(2,1)S(1)} collective-permute-done((bf16[1,16,64,256]{3,2,1,0:T(8,128)(2,1)S(1)}, bf16[1,16,64,256]{3,2,1,0:T(8,128)(2,1)S(1)}, u32[]{:S(2)}, u32[]{:S(2)}) %collective-permute-start.3) | collective-permute-done | bytes 524320 | tf_op jit(solution)/shard_map/ppermute | solution.py:35
  39.6 7.3 %collective-permute-start.4 = (bf16[1,16,64,256]{3,2,1,0:T(8,128)(2,1)}, bf16[1,16,64,256]{3,2,1,0:T(8,128)(2,1)}, u32[]{:S(2)}, u32[]{:S(2)}) collective-permute-start(bf16[1,16,64,256]{3,2,1,0:T(8,128)(2,1)} %fusion.74), channel_id=1, source_target_pairs={{0,16},{8,24},{16,32},{24,40},{32,48},{40,56},{48,64},{56,72},{64,... | collective-permute-start | bytes 1572872 | tf_op jit(solution)/shard_map/ppermute | solution.py:35
  46.9 8.5 %collective-permute-done.4 = bf16[1,16,64,256]{3,2,1,0:T(8,128)(2,1)} collective-permute-done((bf16[1,16,64,256]{3,2,1,0:T(8,128)(2,1)}, bf16[1,16,64,256]{3,2,1,0:T(8,128)(2,1)}, u32[]{:S(2)}, u32[]{:S(2)}) %collective-permute-start.4) | collective-permute-done | bytes 524320 | tf_op jit(solution)/shard_map/ppermute | solution.py:35
  55.4 2.2 fusion.47
  57.6 8.6 %collective-permute-start.5 = (bf16[1,16,64,256]{3,2,1,0:T(8,128)(2,1)}, bf16[1,16,64,256]{3,2,1,0:T(8,128)(2,1)}, u32[]{:S(2)}, u32[]{:S(2)}) collective-permute-start(bf16[1,16,64,256]{3,2,1,0:T(8,128)(2,1)} %fusion.47), channel_id=1, source_target_pairs={{0,32},{8,40},{16,48},{24,56},{32,64},{40,72},{48,80},{56,88},{64,... | collective-permute-start | bytes 1572872 | tf_op jit(solution)/shard_map/ppermute | solution.py:35
  66.2 1.0 copy.151
  67.2 1.5 collective-permute-start.1
  69.9 4.2 %collective-permute-done.5 = bf16[1,16,64,256]{3,2,1,0:T(8,128)(2,1)} collective-permute-done((bf16[1,16,64,256]{3,2,1,0:T(8,128)(2,1)}, bf16[1,16,64,256]{3,2,1,0:T(8,128)(2,1)}, u32[]{:S(2)}, u32[]{:S(2)}) %collective-permute-start.5) | collective-permute-done | bytes 524320 | tf_op jit(solution)/shard_map/ppermute | solution.py:35
  74.1 1.7 add_convert_fusion.2
  75.8 6.7 %collective-permute-start.6 = (bf16[1,16,64,256]{3,2,1,0:T(8,128)(2,1)S(1)}, bf16[1,16,64,256]{3,2,1,0:T(8,128)(2,1)}, u32[]{:S(2)}, u32[]{:S(2)}) collective-permute-start(bf16[1,16,64,256]{3,2,1,0:T(8,128)(2,1)S(1)} %add_convert_fusion.2), channel_id=1, source_target_pairs={{0,64},{8,72},{16,80},{24,88},{32,96},{40,104},{48,112},{56,120},{... | collective-permute-start | bytes 1572872 | tf_op jit(solution)/shard_map/ppermute | solution.py:35
  84.1 3.0 collective-permute-start.2
  87.3 1.3 copy.160
  89.3 1.9 add_add_fusion.2
  91.8 6.2 %fusion.25 = f32[256,1,16,64]{0,3,2,1:T(8,128)} fusion(bf16[256,16,64]{0,2,1:T(8,128)(2,1)} %bitcast.216, f32[16,256]{1,0:T(8,128)} %copy-done.26, f32[256,256]{1,0:T(8,128)} %fusion.79, pred[256,256]{1,0:T(8,128)(4,1)} %iota_compare_fusion, f32[256,1,16,64]{0,3,2,1:T(8,128)S(1)} %convolution_bitcast_fusion.1, f32[256,16]{0,1:T(8,128)S(1)} %copy.153), kind=kOutput, calls=%fused_computation.33 | convolution fusion | flops 810024960 | bytes 2981888 | tf_op jit(solution)/shard_map/jvp()/while/body/eval_jaxpr/gkts,sgkp->tgkp/dot_general | solution.py:61
  98.0 1.6 copy.157
  99.6 7.3 %copy.174 = bf16[256,4,4,512]{3,0,1,2:T(8,128)(2,1)} copy(bf16[256,4,4,512]{0,3,2,1:T(8,128)(2,1)} %bitcast.193) | data formatting | bytes 8388608 | tf_op jit(solution)/shard_map/reshape | solution.py:168
  106.9 5.0 %all-to-all-start = ((bf16[256,4,4,512]{3,0,1,2:T(8,128)(2,1)}), bf16[256,4,4,512]{3,0,1,2:T(8,128)(2,1)}, u32[]{:S(2)}, u32[]{:S(2)}) async-start(bf16[256,4,4,512]{3,0,1,2:T(8,128)(2,1)} %copy.174), calls=%async_computation.1 | async-start | bytes 8388608 | tf_op jit(solution)/shard_map/all_to_all | solution.py:167
  112.0 9.9 %multiply_reduce_fusion.4 = (f32[256]{0:T(256)S(1)}, f32[256]{0:T(256)S(1)}, f32[256,1024]{1,0:T(8,128)S(1)}, f32[256,1024]{1,0:T(8,128)S(1)}) fusion(bf16[256,1024]{1,0:T(8,128)(2,1)S(1)} %copy-done.10, f32[256,1024]{1,0:T(8,128)S(1)} %copy.157, f32[1024]{0:T(1024)} %mul.575, bf16[256,1024]{1,0:T(8,128)(2,1)S(1)} %copy-done.1, f32[1024]{0:T(1024)} %param.15, ...), kind=kOutput, calls=%fused_computation.67 | convolution fusion | flops 4298637312 | bytes 25176064 | tf_op jit(solution)/shard_map/dot_general | solution.py:152
  122.0 2.2 fusion.76
  124.4 49.0 %all-to-all-done = bf16[256,4,4,512]{3,0,1,2:T(8,128)(2,1)} async-done(((bf16[256,4,4,512]{3,0,1,2:T(8,128)(2,1)}), bf16[256,4,4,512]{3,0,1,2:T(8,128)(2,1)}, u32[]{:S(2)}, u32[]{:S(2)}) %all-to-all-start) | async-done | bytes 4194336 | tf_op jit(solution)/shard_map/all_to_all | solution.py:167
  173.4 4.5 %copy.175 = bf16[4,256,4,1,512]{4,1,0,2,3:T(8,128)(2,1)} copy(bf16[4,256,4,1,512]{4,1,2,0,3:T(8,128)(2,1)} %bitcast.69) | data formatting | bytes 8388608 | tf_op jit(solution)/shard_map/all_to_all | solution.py:167
  177.9 9.3 %convert_bitcast_fusion = bf16[4,512,1024]{1,2,0:T(8,128)(2,1)} fusion(bf16[1024,4,512]{2,0,1:T(8,128)(2,1)} %bitcast.201, bf16[1024,1024]{1,0:T(8,128)(2,1)} %all-gather.5.cloned.1.call-done), kind=kOutput, calls=%fused_computation.1 | convolution fusion | flops 4297064448 | bytes 10485760 | tf_op jit(solution)/shard_map/txd,th->xdh/dot_general | solution.py:175
  188.3 9.5 %convolution_convert_fusion = bf16[256,8192]{1,0:T(8,128)(2,1)} fusion(bf16[256,1024]{1,0:T(8,128)(2,1)S(1)} %copy-done.13, bf16[8192,1024]{1,0:T(8,128)(2,1)} %param.16), kind=kOutput, calls=%fused_computation | convolution fusion | flops 4297064448 | bytes 21495808 | tf_op jit(solution)/shard_map/th,dh->td/dot_general | solution.py:145
  197.8 1.2 copy-done.9
  199.1 1.3 copy.161
  200.4 1.8 fusion.52
  203.1 1.3 collective-permute-start.10
  204.4 1.2 copy.166
  205.6 1.3 collective-permute-start.8
  206.9 5.7 %collective-permute-done.8 = f32[1,16]{1,0:T(1,128)S(1)} collective-permute-done((f32[1,16]{1,0:T(1,128)S(1)}, f32[1,16]{1,0:T(1,128)S(1)}, u32[]{:S(2)}, u32[]{:S(2)}) %collective-permute-start.8) | collective-permute-done | bytes 96 | tf_op jit(solution)/shard_map/ppermute | solution.py:34
  212.5 1.3 collective-permute-start.9
  213.8 19.0 %collective-permute-done.9 = f32[1,16]{1,0:T(1,128)S(1)} collective-permute-done((f32[1,16]{1,0:T(1,128)S(1)}, f32[1,16]{1,0:T(1,128)S(1)}, u32[]{:S(2)}, u32[]{:S(2)}) %collective-permute-start.9) | collective-permute-done | bytes 96 | tf_op jit(solution)/shard_map/ppermute | solution.py:34
  233.4 1.6 copy.163
  235.0 2.4 fusion.75
  237.4 1.3 collective-permute-start.11
  238.6 2.0 multiply_reduce_fusion.1
  240.6 1.5 copy.169
  242.1 2.5 convolution_bitcast_fusion.3
  244.6 1.6 fusion.73
  246.2 5.8 %collective-permute-done.11 = bf16[1,16,64,256]{3,2,1,0:T(8,128)(2,1)} collective-permute-done((bf16[1,16,64,256]{3,2,1,0:T(8,128)(2,1)}, bf16[1,16,64,256]{3,2,1,0:T(8,128)(2,1)}, u32[]{:S(2)}, u32[]{:S(2)}) %collective-permute-start.11) | collective-permute-done | bytes 524320 | tf_op jit(solution)/shard_map/ppermute | solution.py:35
  252.0 1.5 fusion.48
  253.5 1.5 collective-permute-start.12
  255.1 5.0 %fusion.7 = (f32[16,256]{1,0:T(8,128)}, f32[16,256]{1,0:T(8,128)S(1)}, f32[256,256]{1,0:T(8,128)S(1)}) fusion(f32[16,256]{1,0:T(8,128)S(1)} %copy-done.27, f32[256,256]{1,0:T(8,128)S(1)} %copy-done.21, pred[256,256]{1,0:T(8,128)(4,1)S(1)} %copy-done.28, f32[16,64,256]{2,1,0:T(8,128)S(1)} %bitcast.198, bf16[256,16,64]{0,2,1:T(8,128)(2,1)S(1)} %bitcast.217), kind=kOutput, calls=%fused_computation.10 | convolution fusion | flops 816766976 | bytes 2211840 | tf_op jit(solution)/shard_map/transpose(jvp())/while/body/eval_jaxpr/gkts,sgkp->tgkp/dot_general | solution.py:61
  260.2 6.4 %collective-permute-done.12 = bf16[1,16,64,256]{3,2,1,0:T(8,128)(2,1)S(1)} collective-permute-done((bf16[1,16,64,256]{3,2,1,0:T(8,128)(2,1)S(1)}, bf16[1,16,64,256]{3,2,1,0:T(8,128)(2,1)S(1)}, u32[]{:S(2)}, u32[]{:S(2)}) %collective-permute-start.12) | collective-permute-done | bytes 524320 | tf_op jit(solution)/shard_map/ppermute | solution.py:35
  266.6 2.7 add_convert_fusion.1
  269.3 1.3 collective-permute-start.13
  270.6 1.0 convolution_bitcast_fusion.2
  273.2 1.9 fusion.33
  275.1 7.4 %collective-permute-done.13 = bf16[1,16,64,256]{3,2,1,0:T(8,128)(2,1)S(1)} collective-permute-done((bf16[1,16,64,256]{3,2,1,0:T(8,128)(2,1)}, bf16[1,16,64,256]{3,2,1,0:T(8,128)(2,1)S(1)}, u32[]{:S(2)}, u32[]{:S(2)}) %collective-permute-start.13) | collective-permute-done | bytes 524320 | tf_op jit(solution)/shard_map/ppermute | solution.py:35
  283.4 2.8 multiply_reduce_fusion.2
  286.2 3.5 %multiply_reduce_fusion.3 = (f32[256,16]{0,1:T(8,128)}, f32[256,1,16,64]{0,3,2,1:T(8,128)}) fusion(f32[256,1,16,64]{0,3,2,1:T(8,128)} %bitcast.200, bf16[256,256]{1,0:T(8,128)(2,1)S(1)} %copy-done, f32[1,16,64,256]{3,2,1,0:T(8,128)S(1)} %get-tuple-element.390), kind=kOutput, calls=%fused_computation.58 | convolution fusion | flops 805826560 | bytes 3293184 | tf_op jit(solution)/shard_map/transpose(jvp())/while/body/eval_jaxpr/sgkp,sgn->gkpn/dot_general | solution.py:66
  289.7 1.5 copy.167
  292.8 1.2 add_add_fusion.3
  294.0 2.5 reduce-window.36
  296.6 2.8 fusion.34
  300.2 5.1 %fusion.28 = f32[256,1,16,64]{0,3,2,1:T(8,128)S(1)} fusion(f32[16,64,256]{2,1,0:T(8,128)S(1)} %bitcast.199, f32[16,256]{1,0:T(8,128)} %copy-done.26, f32[256,256]{1,0:T(8,128)} %fusion.79, pred[256,256]{1,0:T(8,128)(4,1)} %iota_compare_fusion, f32[256,1,16,64]{0,3,2,1:T(8,128)} %get-tuple-element.416, f32[256,16]{0,1:T(8,128)S(1)} %copy-done.25), kind=kOutput, calls=%fused_computation.34 | convolution fusion | flops 810024960 | bytes 3506176 | tf_op jit(solution)/shard_map/transpose(jvp())/while/body/eval_jaxpr/gkts,sgkp->tgkp/dot_general | solution.py:61
  307.3 2.3 copy.178
  (137 shorter events, 19.3 us)
Async XLA Ops:
  7.2 17.6 %copy-start = (bf16[256,256]{1,0:T(8,128)(2,1)S(1)}, bf16[256,256]{1,0:T(8,128)(2,1)}, u32[]{:S(2)}) copy-start(bf16[256,256]{1,0:T(8,128)(2,1)} %param.11) | copy-start | bytes 393220
  7.2 14.7 %copy-start.1 = (bf16[256,1024]{1,0:T(8,128)(2,1)S(1)}, bf16[256,1024]{1,0:T(8,128)(2,1)}, u32[]{:S(2)}) copy-start(bf16[256,1024]{1,0:T(8,128)(2,1)} %param.9) | copy-start | bytes 1572868
  7.2 92.4 %all-gather.3.cloned.1.call-start = ((), (), s32[]{:S(2)}) async-start(), calls=%async_computation.4 | async-start | bytes 4718592 | tf_op jit(solution)/shard_map/all_gather | solution.py:151
  10.9 9.8 %copy-start.26 = (f32[16,256]{1,0:T(8,128)}, f32[16,256]{1,0:T(8,128)S(1)}, u32[]{:S(2)}) copy-start(f32[16,256]{1,0:T(8,128)S(1)} %copy_bitcast_fusion) | copy-start | bytes 49156
  11.1 4.9 %collective-permute-start = (f32[1,16]{1,0:T(1,128)S(1)}, f32[1,16]{1,0:T(1,128)S(1)}, u32[]{:S(2)}, u32[]{:S(2)}) collective-permute-start(f32[1,16]{1,0:T(1,128)S(1)} %slice_exponential_fusion), channel_id=1, source_target_pairs={{0,8},{8,16},{16,24},{24,32},{32,40},{40,48},{48,56},{56,64},{64,7... | collective-permute-start | bytes 200 | tf_op jit(solution)/shard_map/ppermute | solution.py:34
  14.7 5.5 %collective-permute-start.7 = (f32[1,16]{1,0:T(1,128)S(1)}, f32[1,16]{1,0:T(1,128)S(1)}, u32[]{:S(2)}, u32[]{:S(2)}) collective-permute-start(f32[1,16]{1,0:T(1,128)S(1)} %slice_exponential_fusion), channel_id=1, source_target_pairs={{8,0},{16,8},{24,16},{32,24},{40,32},{48,40},{56,48},{64,56},{72,6... | collective-permute-start | bytes 200 | tf_op jit(solution)/shard_map/ppermute | solution.py:34
  21.4 4.0 %copy-start.14 = (f32[256,16]{1,0:T(8,128)}, f32[256,16]{1,0:T(8,128)S(1)}, u32[]{:S(2)}) copy-start(f32[256,16]{1,0:T(8,128)S(1)} %get-tuple-element.407) | copy-start | bytes 49156
  21.5 3.9 %copy-start.24 = (f32[256,16]{0,1:T(8,128)}, f32[256,16]{0,1:T(8,128)S(1)}, u32[]{:S(2)}) copy-start(f32[256,16]{0,1:T(8,128)S(1)} %copy.154) | copy-start | bytes 49156
  24.7 32.8 %copy-start.2 = (f32[256,1024]{0,1:T(8,128)}, f32[256,1024]{0,1:T(8,128)S(1)}, u32[]{:S(2)}) copy-start(f32[256,1024]{0,1:T(8,128)S(1)} %copy.156) | copy-start | bytes 3145732
  25.4 43.3 %copy-start.38 = (f32[16]{0:T(128)S(1)}, f32[16]{0:T(128)}, u32[]{:S(2)}) copy-start(f32[16]{0:T(128)} %param.14) | copy-start | bytes 196
  25.5 13.2 %collective-permute-start.3 = (bf16[1,16,64,256]{3,2,1,0:T(8,128)(2,1)S(1)}, bf16[1,16,64,256]{3,2,1,0:T(8,128)(2,1)S(1)}, u32[]{:S(2)}, u32[]{:S(2)}) collective-permute-start(bf16[1,16,64,256]{3,2,1,0:T(8,128)(2,1)S(1)} %convert_bitcast_fusion.2), channel_id=1, source_target_pairs={{0,8},{8,16},{16,24},{24,32},{32,40},{40,48},{48,56},{56,64},{64,7... | collective-permute-start | bytes 1572872 | tf_op jit(solution)/shard_map/ppermute | solution.py:35
  29.0 46.7 %copy-start.29 = (f32[16]{0:T(128)}, f32[16]{0:T(128)S(1)}, u32[]{:S(2)}) copy-start(f32[16]{0:T(128)S(1)} %fusion.68) | copy-start | bytes 196
  29.0 54.1 %copy-start.12 = (bf16[256,256]{1,0:T(8,128)(2,1)S(1)}, bf16[256,256]{1,0:T(8,128)(2,1)}, u32[]{:S(2)}) copy-start(bf16[256,256]{1,0:T(8,128)(2,1)} %param.12) | copy-start | bytes 393220
  39.6 15.8 %collective-permute-start.4 = (bf16[1,16,64,256]{3,2,1,0:T(8,128)(2,1)}, bf16[1,16,64,256]{3,2,1,0:T(8,128)(2,1)}, u32[]{:S(2)}, u32[]{:S(2)}) collective-permute-start(bf16[1,16,64,256]{3,2,1,0:T(8,128)(2,1)} %fusion.74), channel_id=1, source_target_pairs={{0,16},{8,24},{16,32},{24,40},{32,48},{40,56},{48,64},{56,72},{64,... | collective-permute-start | bytes 1572872 | tf_op jit(solution)/shard_map/ppermute | solution.py:35
  57.6 16.5 %collective-permute-start.5 = (bf16[1,16,64,256]{3,2,1,0:T(8,128)(2,1)}, bf16[1,16,64,256]{3,2,1,0:T(8,128)(2,1)}, u32[]{:S(2)}, u32[]{:S(2)}) collective-permute-start(bf16[1,16,64,256]{3,2,1,0:T(8,128)(2,1)} %fusion.47), channel_id=1, source_target_pairs={{0,32},{8,40},{16,48},{24,56},{32,64},{40,72},{48,80},{56,88},{64,... | collective-permute-start | bytes 1572872 | tf_op jit(solution)/shard_map/ppermute | solution.py:35
  66.2 17.9 %copy-start.20 = (f32[256,16]{1,0:T(8,128)S(1)}, f32[256,16]{1,0:T(8,128)}, u32[]{:S(2)}) copy-start(f32[256,16]{1,0:T(8,128)} %get-tuple-element.406) | copy-start | bytes 49156
  66.2 23.1 %copy-start.35 = (f32[1,16]{1,0:T(1,128)S(1)}, f32[1,16]{1,0:T(1,128)}, u32[]{:S(2)}) copy-start(f32[1,16]{1,0:T(1,128)} %get-tuple-element.403) | copy-start | bytes 196
  67.2 2.7 collective-permute-start.1
  75.8 13.5 %collective-permute-start.6 = (bf16[1,16,64,256]{3,2,1,0:T(8,128)(2,1)S(1)}, bf16[1,16,64,256]{3,2,1,0:T(8,128)(2,1)}, u32[]{:S(2)}, u32[]{:S(2)}) collective-permute-start(bf16[1,16,64,256]{3,2,1,0:T(8,128)(2,1)S(1)} %add_convert_fusion.2), channel_id=1, source_target_pairs={{0,64},{8,72},{16,80},{24,88},{32,96},{40,104},{48,112},{56,120},{... | collective-permute-start | bytes 1572872 | tf_op jit(solution)/shard_map/ppermute | solution.py:35
  84.1 5.2 %collective-permute-start.2 = (f32[1,16]{1,0:T(1,128)S(1)}, f32[1,16]{1,0:T(1,128)S(1)}, u32[]{:S(2)}, u32[]{:S(2)}) collective-permute-start(f32[1,16]{1,0:T(1,128)S(1)} %fusion.63), channel_id=1, source_target_pairs={{0,32},{8,40},{16,48},{24,56},{32,64},{40,72},{48,80},{56,88},{64,... | collective-permute-start | bytes 200 | tf_op jit(solution)/shard_map/ppermute | solution.py:34
  91.8 6.2 %copy-start.7 = (f32[256,1,16,64]{0,3,2,1:T(8,128)}, f32[256,1,16,64]{0,3,2,1:T(8,128)S(1)}, u32[]{:S(2)}) copy-start(f32[256,1,16,64]{0,3,2,1:T(8,128)S(1)} %convolution_bitcast_fusion.1) | copy-start | bytes 3145732
  106.9 5.1 %copy-start.10 = (bf16[256,1024]{1,0:T(8,128)(2,1)S(1)}, bf16[256,1024]{1,0:T(8,128)(2,1)}, u32[]{:S(2)}) copy-start(bf16[256,1024]{1,0:T(8,128)(2,1)} %param.10) | copy-start | bytes 1572868
  106.9 66.5 %all-to-all-start = ((bf16[256,4,4,512]{3,0,1,2:T(8,128)(2,1)}), bf16[256,4,4,512]{3,0,1,2:T(8,128)(2,1)}, u32[]{:S(2)}, u32[]{:S(2)}) async-start(bf16[256,4,4,512]{3,0,1,2:T(8,128)(2,1)} %copy.174), calls=%async_computation.1 | async-start | bytes 8388608 | tf_op jit(solution)/shard_map/all_to_all | solution.py:167
  111.9 66.0 %all-gather.5.cloned.1.call-start = ((), (), s32[]{:S(2)}) async-start(), calls=%async_computation.5 | async-start | bytes 2621440 | tf_op jit(solution)/shard_map/all_gather | solution.py:174
  112.0 10.0 %copy-start.8 = (f32[256,1024]{1,0:T(8,128)S(1)}, f32[256,1024]{1,0:T(8,128)}, u32[]{:S(2)}) copy-start(f32[256,1024]{1,0:T(8,128)} %copy.160) | copy-start | bytes 3145732
  112.0 10.0 %copy-start.22 = (f32[1024]{0:T(1024)S(1)}, f32[1024]{0:T(1024)}, u32[]{:S(2)}) copy-start(f32[1024]{0:T(1024)} %mul.575) | copy-start | bytes 12292
  112.0 10.0 %copy-start.31 = (f32[1024]{0:T(1024)S(1)}, f32[1024]{0:T(1024)}, u32[]{:S(2)}) copy-start(f32[1024]{0:T(1024)} %param.15) | copy-start | bytes 12292
  124.2 183.1 %reduce-scatter.5.cloned.1.call-start = ((), (), s32[]{:S(2)}) async-start(), calls=%async_computation.6 | async-start | bytes 5242880 | tf_op jit(solution)/shard_map/reduce_scatter | solution.py:178
  187.3 1.0 copy-start.13
  187.3 122.3 %reduce-scatter.3.cloned.1.call-start = ((), (), s32[]{:S(2)}) async-start(), calls=%async_computation.3 | async-start | bytes 4718592 | tf_op jit(solution)/shard_map/reduce_scatter | solution.py:148
  197.8 1.3 copy-start.9
  197.8 7.7 %copy-start.32 = (f32[1,16]{1,0:T(1,128)S(1)}, f32[1,16]{1,0:T(1,128)}, u32[]{:S(2)}) copy-start(f32[1,16]{1,0:T(1,128)} %get-tuple-element.391) | copy-start | bytes 196
  197.8 35.0 %copy-start.34 = (f32[1,16]{1,0:T(1,128)S(1)}, f32[1,16]{1,0:T(1,128)}, u32[]{:S(2)}) copy-start(f32[1,16]{1,0:T(1,128)} %get-tuple-element.392) | copy-start | bytes 196
  203.1 31.9 %collective-permute-start.10 = (bf16[1,16,64,256]{3,2,1,0:T(8,128)(2,1)}, bf16[1,16,64,256]{3,2,1,0:T(8,128)(2,1)}, u32[]{:S(2)}, u32[]{:S(2)}) collective-permute-start(bf16[1,16,64,256]{3,2,1,0:T(8,128)(2,1)} %convert_bitcast_fusion.1), channel_id=1, source_target_pairs={{8,0},{16,8},{24,16},{32,24},{40,32},{48,40},{56,48},{64,56},{72,6... | collective-permute-start | bytes 1572872 | tf_op jit(solution)/shard_map/ppermute | solution.py:35
  205.6 7.0 %collective-permute-start.8 = (f32[1,16]{1,0:T(1,128)S(1)}, f32[1,16]{1,0:T(1,128)S(1)}, u32[]{:S(2)}, u32[]{:S(2)}) collective-permute-start(f32[1,16]{1,0:T(1,128)S(1)} %copy-done.32), channel_id=1, source_target_pairs={{16,0},{24,8},{32,16},{40,24},{48,32},{56,40},{64,48},{72,56},{80,... | collective-permute-start | bytes 200 | tf_op jit(solution)/shard_map/ppermute | solution.py:34
  212.5 20.8 %copy-start.36 = (f32[1,16]{1,0:T(1,128)}, f32[1,16]{1,0:T(1,128)S(1)}, u32[]{:S(2)}) copy-start(f32[1,16]{1,0:T(1,128)S(1)} %fusion.65) | copy-start | bytes 196
  212.5 20.3 %collective-permute-start.9 = (f32[1,16]{1,0:T(1,128)S(1)}, f32[1,16]{1,0:T(1,128)S(1)}, u32[]{:S(2)}, u32[]{:S(2)}) collective-permute-start(f32[1,16]{1,0:T(1,128)S(1)} %fusion.65), channel_id=1, source_target_pairs={{32,0},{40,8},{48,16},{56,24},{64,32},{72,40},{80,48},{88,56},{96,... | collective-permute-start | bytes 200 | tf_op jit(solution)/shard_map/ppermute | solution.py:34
  234.9 20.1 %copy-start.4 = (f32[256,1024]{0,1:T(8,128)}, f32[256,1024]{0,1:T(8,128)S(1)}, u32[]{:S(2)}) copy-start(f32[256,1024]{0,1:T(8,128)S(1)} %copy.163) | copy-start | bytes 3145732
  237.4 14.6 %collective-permute-start.11 = (bf16[1,16,64,256]{3,2,1,0:T(8,128)(2,1)}, bf16[1,16,64,256]{3,2,1,0:T(8,128)(2,1)}, u32[]{:S(2)}, u32[]{:S(2)}) collective-permute-start(bf16[1,16,64,256]{3,2,1,0:T(8,128)(2,1)} %fusion.75), channel_id=1, source_target_pairs={{16,0},{24,8},{32,16},{40,24},{48,32},{56,40},{64,48},{72,56},{80,... | collective-permute-start | bytes 1572872 | tf_op jit(solution)/shard_map/ppermute | solution.py:35
  242.1 13.0 %copy-start.19 = (bf16[256,1024]{0,1:T(8,128)(2,1)S(1)}, bf16[256,1024]{0,1:T(8,128)(2,1)}, u32[]{:S(2)}) copy-start(bf16[256,1024]{0,1:T(8,128)(2,1)} %copy.151) | copy-start | bytes 1572868
  242.1 13.0 %copy-start.21 = (f32[256,256]{1,0:T(8,128)S(1)}, f32[256,256]{1,0:T(8,128)}, u32[]{:S(2)}) copy-start(f32[256,256]{1,0:T(8,128)} %fusion.79) | copy-start | bytes 786436
  242.1 13.0 %copy-start.27 = (f32[16,256]{1,0:T(8,128)S(1)}, f32[16,256]{1,0:T(8,128)}, u32[]{:S(2)}) copy-start(f32[16,256]{1,0:T(8,128)} %copy-done.26) | copy-start | bytes 49156
  242.1 13.0 %copy-start.28 = (pred[256,256]{1,0:T(8,128)(4,1)S(1)}, pred[256,256]{1,0:T(8,128)(4,1)}, u32[]{:S(2)}) copy-start(pred[256,256]{1,0:T(8,128)(4,1)} %iota_compare_fusion) | copy-start | bytes 196612
  253.5 13.1 %collective-permute-start.12 = (bf16[1,16,64,256]{3,2,1,0:T(8,128)(2,1)S(1)}, bf16[1,16,64,256]{3,2,1,0:T(8,128)(2,1)S(1)}, u32[]{:S(2)}, u32[]{:S(2)}) collective-permute-start(bf16[1,16,64,256]{3,2,1,0:T(8,128)(2,1)S(1)} %fusion.48), channel_id=1, source_target_pairs={{32,0},{40,8},{48,16},{56,24},{64,32},{72,40},{80,48},{88,56},{96,... | collective-permute-start | bytes 1572872 | tf_op jit(solution)/shard_map/ppermute | solution.py:35
  255.1 11.5 %copy-start.30 = (f32[16]{0:T(128)S(1)}, f32[16]{0:T(128)}, u32[]{:S(2)}) copy-start(f32[16]{0:T(128)} %copy-done.29) | copy-start | bytes 196
  255.1 11.5 %copy-start.33 = (f32[1,16]{1,0:T(1,128)S(1)}, f32[1,16]{1,0:T(1,128)}, u32[]{:S(2)}) copy-start(f32[1,16]{1,0:T(1,128)} %get-tuple-element.391) | copy-start | bytes 196
  255.1 11.5 %copy-start.37 = (f32[1,16]{1,0:T(1,128)S(1)}, f32[1,16]{1,0:T(1,128)}, u32[]{:S(2)}) copy-start(f32[1,16]{1,0:T(1,128)} %copy-done.36) | copy-start | bytes 196
  260.2 11.5 %copy-start.17 = (f32[256,256]{1,0:T(8,128)}, f32[256,256]{1,0:T(8,128)S(1)}, u32[]{:S(2)}) copy-start(f32[256,256]{1,0:T(8,128)S(1)} %get-tuple-element.386) | copy-start | bytes 786436
  260.2 13.0 %copy-start.16 = (f32[256,256]{1,0:T(8,128)S(1)}, f32[256,256]{1,0:T(8,128)}, u32[]{:S(2)}) copy-start(f32[256,256]{1,0:T(8,128)} %convolution_bitcast_fusion.3) | copy-start | bytes 786436
  266.6 2.7 copy-start.11
  269.3 13.2 %collective-permute-start.13 = (bf16[1,16,64,256]{3,2,1,0:T(8,128)(2,1)}, bf16[1,16,64,256]{3,2,1,0:T(8,128)(2,1)S(1)}, u32[]{:S(2)}, u32[]{:S(2)}) collective-permute-start(bf16[1,16,64,256]{3,2,1,0:T(8,128)(2,1)} %add_convert_fusion.1), channel_id=1, source_target_pairs={{64,0},{72,8},{80,16},{88,24},{96,32},{104,40},{112,48},{120,56},{... | collective-permute-start | bytes 1572872 | tf_op jit(solution)/shard_map/ppermute | solution.py:35
  273.2 18.0 %copy-start.15 = (f32[256,16]{1,0:T(8,128)S(1)}, f32[256,16]{1,0:T(8,128)}, u32[]{:S(2)}) copy-start(f32[256,16]{1,0:T(8,128)} %copy-done.14) | copy-start | bytes 49156
  282.6 0.8 copy-start.18
  283.4 13.3 %copy-start.3 = (f32[256,1024]{0,1:T(8,128)S(1)}, f32[256,1024]{0,1:T(8,128)}, u32[]{:S(2)}) copy-start(f32[256,1024]{0,1:T(8,128)} %copy-done.2) | copy-start | bytes 3145732
  286.2 14.0 %copy-start.5 = (f32[256,1024]{0,1:T(8,128)S(1)}, f32[256,1024]{0,1:T(8,128)}, u32[]{:S(2)}) copy-start(f32[256,1024]{0,1:T(8,128)} %copy-done.4) | copy-start | bytes 3145732
  286.2 14.0 %copy-start.25 = (f32[256,16]{0,1:T(8,128)S(1)}, f32[256,16]{0,1:T(8,128)}, u32[]{:S(2)}) copy-start(f32[256,16]{0,1:T(8,128)} %copy-done.24) | copy-start | bytes 49156
  300.2 6.1 %copy-start.6 = (f32[256,1024]{1,0:T(8,128)S(1)}, f32[256,1024]{1,0:T(8,128)}, u32[]{:S(2)}) copy-start(f32[256,1024]{1,0:T(8,128)} %get-tuple-element.394) | copy-start | bytes 3145732
  300.2 6.1 %copy-start.23 = (f32[1024]{0:T(1024)S(1)}, f32[1024]{0:T(1024)}, u32[]{:S(2)}) copy-start(f32[1024]{0:T(1024)} %mul.575) | copy-start | bytes 12292
Sparse Core Ops, SparseCore 0:
  10.3 34.7 all-gather.2
  124.3 47.5 all-gather.4
  187.4 60.3 reduce-scatter.4
  250.7 36.6 reduce-scatter.2

commit v4 on v3

--- a/solution.py
+++ b/solution.py
@@ -4,6 +4,7 @@
 import jax.numpy as jnp
 from jax import lax
 from jax.sharding import Mesh, PartitionSpec as P
+
 
 HALF_HEADS = 128
 P_SIZE = 64
@@ -17,7 +18,7 @@
 highest = lax.Precision.HIGHEST
 
 
-def log_scan(x, axis, reverse):
+def log_scan(x, axis, reverse, before_send=None, after_receive=None):
     count = lax.axis_size(axis)
     place = lax.axis_index(axis)
     decay, state = x
@@ -31,8 +32,12 @@
         else:
             pairs = [(i, i + hop) for i in range(count - hop)]
             valid = place >= hop
+        if before_send is not None:
+            incl = (incl[0], before_send(hop, incl[1]))
         got_decay = lax.ppermute(incl[0], axis, pairs)
         got_state = lax.ppermute(incl[1].astype(jnp.bfloat16), axis, pairs).astype(jnp.float32)
+        if after_receive is not None:
+            got_state = after_receive(hop, got_state)
         got_decay = jnp.where(valid, got_decay, 1.0)
         got_state = jnp.where(valid, got_state, 0.0)
         excl = (got_decay * excl[0], excl[0][..., None, None] * got_state + excl[1])
@@ -105,10 +110,6 @@
     grouped = gated_vals.reshape(row_count, -1, HALF_HEADS * P_SIZE // G)
     factor = lax.rsqrt(jnp.mean(grouped * grouped, axis=2, keepdims=True) + epsilon)
     return (grouped * factor).reshape(row_count, head_count * P_SIZE) * norm_gain
-
-
-def combine(earlier, later):
-    return (earlier[0] * later[0], later[0][..., None, None] * earlier[1] + later[1])
 
 
 def per_device(
@@ -130,12 +131,41 @@
     writes = write_vectors.astype(jnp.float32)
     reading = read_vectors.astype(jnp.float32)
     zero_state = jnp.zeros((group_count, per_group, P_SIZE, N), jnp.float32)
-    own_state, unused = lax.scan(
+    own_state, _ = lax.scan(
         block_end, zero_state, (in_blocks(inputs), in_blocks(writes), in_blocks(log_decay))
     )
     cumulative = jnp.cumsum(log_decay, axis=0)
     own_decay = jnp.exp(cumulative[-1]).reshape(group_count, per_group)
-    decay_before, start_state = log_scan((own_decay, own_state), SEQ, False)
+    rows = lax.axis_size("sx")
+    cols = lax.axis_size("sy")
+    full_grad = lax.all_gather(out_grad, "head", axis=1, tiled=True)
+    feature_count = full_grad.shape[1]
+    block = feature_count // (rows * cols)
+    tied = {}
+
+    def during_forward(hop, state):
+        if hop == 4:
+            state, tied["grad"] = lax.optimization_barrier((state, full_grad))
+        if hop == 8:
+            columns = lax.all_to_all(
+                tied["grad"].reshape(row_count, rows, cols, block),
+                "sy",
+                split_axis=2,
+                concat_axis=0,
+                tiled=True,
+            ).reshape(cols * row_count, rows, block)
+            normed_grad = jnp.dot(tied["grad"], out_weight, preferred_element_type=jnp.float32)
+            state, tied["columns"], tied["normed_grad"] = lax.optimization_barrier(
+                (state, columns, normed_grad)
+            )
+        return state
+
+    def during_backward(hop, got_state):
+        if hop == 2:
+            got_state, tied["late_normed"] = lax.optimization_barrier((got_state, normed_half))
+        return got_state
+
+    _, start_state = log_scan((own_decay, own_state), SEQ, False, during_forward)
     (ssd_out, end_state), ssd_pull = jax.vjp(
         ssd_run, inputs, writes, reading, log_decay, start_state
     )
@@ -148,32 +178,19 @@
     layer_out = lax.psum_scatter(
         partial_out.astype(jnp.bfloat16), "head", scatter_dimension=1, tiled=True
     )
-    full_grad = lax.all_gather(out_grad, "head", axis=1, tiled=True)
-    normed_grad = jnp.dot(full_grad, out_weight, preferred_element_type=jnp.float32)
-    ssd_grad, skip_input_grad, gate_grad = norm_pull(normed_grad)
+    ssd_grad, skip_input_grad, gate_grad = norm_pull(tied["normed_grad"])
     scaled_grad = ssd_grad.reshape(row_count, group_count, per_group, P_SIZE) * jnp.exp(
         cumulative
     ).reshape(row_count, group_count, per_group, 1)
     state_direct = jnp.einsum(
         "tgkp,tgn->gkpn", scaled_grad, reading.reshape(row_count, group_count, N), precision=highest
     )
-    decay_after, end_grad = log_scan((own_decay, state_direct), SEQ, True)
-    input_part, write_grad, read_grad, decay_grad, start_grad = ssd_pull((ssd_grad, end_grad))
+    _, end_grad = log_scan((own_decay, state_direct), SEQ, True, after_receive=during_backward)
+    input_part, write_grad, read_grad, decay_grad, _ = ssd_pull((ssd_grad, end_grad))
     input_grad = skip_input_grad + input_part
-    rows = lax.axis_size("sx")
-    cols = lax.axis_size("sy")
-    feature_count = full_grad.shape[1]
-    block = feature_count // (rows * cols)
-    grad_columns = lax.all_to_all(
-        full_grad.reshape(row_count, rows, cols, block),
-        "sy",
-        split_axis=2,
-        concat_axis=0,
-        tiled=True,
-    ).reshape(cols * row_count, rows, block)
-    row_normed = lax.all_gather(normed_half, "sy", axis=0, tiled=True)
+    row_normed = lax.all_gather(tied["late_normed"], "sy", axis=0, tiled=True)
     row_partial = jnp.einsum(
-        "txd,th->xdh", grad_columns, row_normed, preferred_element_type=jnp.float32
+        "txd,th->xdh", tied["columns"], row_normed, preferred_element_type=jnp.float32
     ).astype(jnp.bfloat16)
     weight_grad = lax.psum_scatter(row_partial, "sx", scatter_dimension=0, tiled=True).reshape(
         block, row_normed.shape[1]

time: 319 us -> 348 us (1.091)
  waiting for transfers between devices: 121 us -> 146 us
  starting transfers between devices: 48.8 us -> 55.8 us
    all_to_all x1, waiting for transfers between devices: 49 us -> 0.01 us  [during_forward(): lax.all_to_all(tied['grad'].reshape(row_count, rows, cols, block), 'sy',...]
    all_gather x1, waiting for transfers between devices: 0.01 us -> 29 us  [per_device(): row_normed = lax.all_gather(tied['late_normed'], 'sy', axis=0, tiled=True)]
    ppermute x8, waiting for transfers between devices: 41.9 us -> 70.4 us  [log_scan(): lax.ppermute(incl[1].astype(jnp.bfloat16), axis, pairs).astype(jnp.float32)]
    ppermute x6, waiting for transfers between devices: 30.1 us -> 46.5 us  [log_scan(): got_decay = lax.ppermute(incl[0], axis, pairs)]
    convert_element_type x8 -> x7, other arithmetic: 12.3 us -> 5.25 us  [log_scan(): incl[1].astype(jnp.bfloat16)]
    all_to_all x1 -> x0, local copies, waits for them, and re-layouts: 4.53 us -> none  [per_device(): lax.all_to_all(full_grad.reshape(row_count, rows, cols, block), 'sy', spl...]
    ppermute x6, starting transfers between devices: 11.9 us -> 16.2 us  [log_scan(): got_decay = lax.ppermute(incl[0], axis, pairs)]
    all_to_all x1, starting transfers between devices: 5 us -> 8.54 us  [during_forward(): lax.all_to_all(tied['grad'].reshape(row_count, rows, cols, block), 'sy',...]
  transfers between devices with their start and end apart: 19 -> 19, of which waited for: 12 -> 12; matrix products, arithmetic and copies ran while one was open for 35% -> 29% of each run, Pallas kernels for 0% -> 0%
where the time goes in v4:
time: 348 us; the launch traced here: 346 us
  waiting for transfers between devices  146 us (42%)
  matrix products  58.2 us (17%)
  starting transfers between devices  55.8 us (16%)
  local copies, waits for them, and re-layouts  36 us (10%)
  other arithmetic  35.8 us (10%)
  between operations  14.4 us (4%)
    ppermute x8, waiting for transfers between devices, log_scan(): lax.ppermute(incl[1].astype(jnp.bfloat16), axis, pairs).astype(jnp.float32)  70.4 us
    ppermute x6, waiting for transfers between devices, log_scan(): got_decay = lax.ppermute(incl[0], axis, pairs)  46.5 us
    ppermute x8, starting transfers between devices, log_scan(): lax.ppermute(incl[1].astype(jnp.bfloat16), axis, pairs).astype(jnp.float32)  30.7 us
    all_gather x1, waiting for transfers between devices, per_device(): row_normed = lax.all_gather(tied['late_normed'], 'sy', axis=0, tiled=True)  29 us
    ppermute x6, starting transfers between devices, log_scan(): got_decay = lax.ppermute(incl[0], axis, pairs)  16.2 us
    dot_general x3, matrix products, block_scan(): jnp.einsum('gkts,sgkp->tgkp', weights, input_heads, precision=highest)  14.3 us
    dot_general x1, matrix products, per_device(): jnp.einsum('th,dh->td', normed_half, out_weight, preferred_element_type=j...  9.73 us
    dot_general x1, matrix products, per_device(): jnp.einsum('txd,th->xdh', tied['columns'], row_normed, preferred_element_...  9.66 us
  transfers between devices with their start and end apart: 19, of which 12 were waited for; matrix products, arithmetic and copies ran while one was open for 29% of the time, Pallas kernels for 0%

profile of v4, /device:TPU:0, one launch (start us, length us, event | category | flops | bytes accessed | tf_op | source)
XLA Modules:
  0.0 346.1 jit_solution(8270013744857003305)
XLA Ops:
  7.2 2.1 copy.145
  11.1 1.3 collective-permute-start.7
  12.4 4.5 %collective-permute-start = (f32[1,16]{1,0:T(1,128)S(1)}, f32[1,16]{1,0:T(1,128)S(1)}, u32[]{:S(2)}, u32[]{:S(2)}) collective-permute-start(f32[1,16]{1,0:T(1,128)S(1)} %slice_exponential_fusion), channel_id=1, source_target_pairs={{0,8},{8,16},{16,24},{24,32},{32,40},{40,48},{48,56},{56,64},{64,7... | collective-permute-start | bytes 200 | tf_op jit(solution)/shard_map/ppermute | solution.py:37
  16.9 1.3 collective-permute-done
  20.4 1.1 convert_multiply_fusion.2
  21.5 1.6 copy.144
  23.9 4.2 %collective-permute-start.3 = (bf16[1,16,64,256]{3,2,1,0:T(8,128)(2,1)S(1)}, bf16[1,16,64,256]{3,2,1,0:T(8,128)(2,1)S(1)}, u32[]{:S(2)}, u32[]{:S(2)}) collective-permute-start(bf16[1,16,64,256]{3,2,1,0:T(8,128)(2,1)S(1)} %convert_bitcast_fusion.1), channel_id=1, source_target_pairs={{0,8},{8,16},{16,24},{24,32},{32,40},{40,48},{48,56},{56,64},{64,7... | collective-permute-start | bytes 1572872 | tf_op jit(solution)/shard_map/ppermute | solution.py:38
  28.1 9.6 %collective-permute-done.3 = bf16[1,16,64,256]{3,2,1,0:T(8,128)(2,1)S(1)} collective-permute-done((bf16[1,16,64,256]{3,2,1,0:T(8,128)(2,1)S(1)}, bf16[1,16,64,256]{3,2,1,0:T(8,128)(2,1)S(1)}, u32[]{:S(2)}, u32[]{:S(2)}) %collective-permute-start.3) | collective-permute-done | bytes 524320 | tf_op jit(solution)/shard_map/ppermute | solution.py:38
  38.7 7.5 %collective-permute-start.4 = (bf16[1,16,64,256]{3,2,1,0:T(8,128)(2,1)}, bf16[1,16,64,256]{3,2,1,0:T(8,128)(2,1)}, u32[]{:S(2)}, u32[]{:S(2)}) collective-permute-start(bf16[1,16,64,256]{3,2,1,0:T(8,128)(2,1)} %fusion.52), channel_id=1, source_target_pairs={{0,16},{8,24},{16,32},{24,40},{32,48},{40,56},{48,64},{56,72},{64,... | collective-permute-start | bytes 1572872 | tf_op jit(solution)/shard_map/ppermute | solution.py:38
  46.2 8.7 %collective-permute-done.4 = bf16[1,16,64,256]{3,2,1,0:T(8,128)(2,1)} collective-permute-done((bf16[1,16,64,256]{3,2,1,0:T(8,128)(2,1)}, bf16[1,16,64,256]{3,2,1,0:T(8,128)(2,1)}, u32[]{:S(2)}, u32[]{:S(2)}) %collective-permute-start.4) | collective-permute-done | bytes 524320 | tf_op jit(solution)/shard_map/ppermute | solution.py:38
  54.9 2.3 multiply_add_fusion.3
  57.2 7.9 %copy.146 = bf16[256,4,4,512]{3,1,0,2:T(4,128)(2,1)} copy(bf16[256,4,4,512]{0,3,2,1:T(8,128)(2,1)} %bitcast.191) | data formatting | bytes 8388608 | tf_op jit(solution)/shard_map/reshape | solution.py:151
  65.2 8.5 %all-to-all-start = ((bf16[256,4,4,512]{3,1,0,2:T(4,128)(2,1)}), bf16[256,4,4,512]{3,1,0,2:T(4,128)(2,1)}, u32[]{:S(2)}, u32[]{:S(2)}) async-start(bf16[256,4,4,512]{3,1,0,2:T(4,128)(2,1)} %copy.146), calls=%async_computation | async-start | bytes 8388608 | tf_op jit(solution)/shard_map/all_to_all | solution.py:150
  73.7 1.0 copy.139
  74.7 5.5 %collective-permute-start.1 = (f32[1,16]{1,0:T(1,128)S(1)}, f32[1,16]{1,0:T(1,128)S(1)}, u32[]{:S(2)}, u32[]{:S(2)}) collective-permute-start(f32[1,16]{1,0:T(1,128)S(1)} %get-tuple-element.416), channel_id=1, source_target_pairs={{0,16},{8,24},{16,32},{24,40},{32,48},{40,56},{48,64},{56,72},{64,... | collective-permute-start | bytes 200 | tf_op jit(solution)/shard_map/ppermute | solution.py:37
  81.0 34.8 %collective-permute-done.1 = f32[1,16]{1,0:T(1,128)S(1)} collective-permute-done((f32[1,16]{1,0:T(1,128)S(1)}, f32[1,16]{1,0:T(1,128)S(1)}, u32[]{:S(2)}, u32[]{:S(2)}) %collective-permute-start.1) | collective-permute-done | bytes 96 | tf_op jit(solution)/shard_map/ppermute | solution.py:37
  116.5 7.9 %collective-permute-start.5 = (bf16[1,16,64,256]{3,2,1,0:T(8,128)(2,1)S(1)}, bf16[1,16,64,256]{3,2,1,0:T(8,128)(2,1)S(1)}, u32[]{:S(2)}, u32[]{:S(2)}) collective-permute-start(bf16[1,16,64,256]{3,2,1,0:T(8,128)(2,1)S(1)} %convert_element_type.98), channel_id=1, source_target_pairs={{0,32},{8,40},{16,48},{24,56},{32,64},{40,72},{48,80},{56,88},{64,... | collective-permute-start | bytes 1572872 | tf_op jit(solution)/shard_map/ppermute | solution.py:38
  124.4 9.4 %fusion.84 = f32[256,1024]{1,0:T(8,128)S(1)} fusion(bf16[256,8192]{0,1:T(8,128)(2,1)} %all-gather.3.cloned.1.call-done, bf16[8192,1024]{1,0:T(8,128)(2,1)} %param.16), kind=kOutput, calls=%fused_computation.137 | convolution fusion | flops 4294967296 | bytes 22020096 | tf_op jit(solution)/shard_map/dot_general | solution.py:157
  135.6 5.7 %collective-permute-start.6 = (bf16[1,16,64,256]{3,2,1,0:T(8,128)(2,1)}, bf16[1,16,64,256]{3,2,1,0:T(8,128)(2,1)}, u32[]{:S(2)}, u32[]{:S(2)}) collective-permute-start(bf16[1,16,64,256]{3,2,1,0:T(8,128)(2,1)} %multiply_add_fusion.2), channel_id=1, source_target_pairs={{0,64},{8,72},{16,80},{24,88},{32,96},{40,104},{48,112},{56,120},{... | collective-permute-start | bytes 1572872 | tf_op jit(solution)/shard_map/ppermute | solution.py:38
  143.8 2.3 collective-permute-start.2
  146.2 1.3 copy.149
  148.6 1.9 add_add_fusion.2
  151.2 4.6 %fusion.30 = f32[256,1,16,64]{0,3,2,1:T(8,128)} fusion(bf16[256,16,64]{0,2,1:T(8,128)(2,1)S(1)} %bitcast.212, f32[16,256]{1,0:T(8,128)S(1)} %copy-done.29, f32[256,256]{1,0:T(8,128)S(1)} %copy-done.23, pred[256,256]{1,0:T(8,128)(4,1)S(1)} %copy-done.32, f32[256,1,16,64]{0,3,2,1:T(8,128)S(1)} %convolution_bitcast_fusion.1, f32[256,16]{0,1:T(8,128)S(1)} %copy.141), kind=kOutput, calls=%fused_computation.34 | convolution fusion | flops 810024960 | bytes 2981888 | tf_op jit(solution)/shard_map/jvp()/while/body/eval_jaxpr/gkts,sgkp->tgkp/dot_general | solution.py:66
  155.8 2.6 copy.147
  158.4 2.0 multiply_reduce_fusion.4
  160.4 2.2 fusion.80
  162.6 1.6 copy.150
  164.8 1.3 collective-permute-start.10
  166.1 9.8 %collective-permute-done.10 = bf16[1,16,64,256]{3,2,1,0:T(8,128)(2,1)S(1)} collective-permute-done((bf16[1,16,64,256]{3,2,1,0:T(8,128)(2,1)S(1)}, bf16[1,16,64,256]{3,2,1,0:T(8,128)(2,1)S(1)}, u32[]{:S(2)}, u32[]{:S(2)}) %collective-permute-start.10) | collective-permute-done | bytes 524320 | tf_op jit(solution)/shard_map/ppermute | solution.py:38
  176.7 1.3 collective-permute-start.11
  178.0 11.8 %collective-permute-done.11 = bf16[1,16,64,256]{3,2,1,0:T(8,128)(2,1)S(1)} collective-permute-done((bf16[1,16,64,256]{3,2,1,0:T(8,128)(2,1)S(1)}, bf16[1,16,64,256]{3,2,1,0:T(8,128)(2,1)S(1)}, u32[]{:S(2)}, u32[]{:S(2)}) %collective-permute-start.11) | collective-permute-done | bytes 524320 | tf_op jit(solution)/shard_map/ppermute | solution.py:38
  190.0 9.7 %convolution_convert_fusion = bf16[256,8192]{1,0:T(8,128)(2,1)} fusion(bf16[256,1024]{1,0:T(8,128)(2,1)} %get-tuple-element.348, bf16[8192,1024]{1,0:T(8,128)(2,1)} %param.16), kind=kOutput, calls=%fused_computation | convolution fusion | flops 4297064448 | bytes 21495808 | tf_op jit(solution)/shard_map/th,dh->td/dot_general | solution.py:175
  200.0 29.0 %all-gather.5.cloned.1.call-done = bf16[1024,1024]{1,0:T(8,128)(2,1)} async-done(((bf16[256,1024]{1,0:T(8,128)(2,1)}), bf16[1024,1024]{1,0:T(8,128)(2,1)}) %all-gather.5.cloned.1.call-update) | async-done | bytes 2097168 | tf_op jit(solution)/shard_map/all_gather | solution.py:191
  229.0 9.7 %fusion.8 = bf16[4,512,1024]{2,1,0:T(8,128)(2,1)} fusion(bf16[1024,4,512]{2,1,0:T(4,128)(2,1)} %bitcast.19, bf16[1024,1024]{1,0:T(8,128)(2,1)} %all-gather.5.cloned.1.call-done), kind=kOutput, calls=%fused_computation.10 | convolution fusion | flops 4297064448 | bytes 10485760 | tf_op jit(solution)/shard_map/txd,th->xdh/dot_general | solution.py:192
  238.7 2.3 copy.155
  240.9 1.3 collective-permute-start.8
  242.2 5.8 %collective-permute-done.8 = f32[1,16]{1,0:T(1,128)} collective-permute-done((f32[1,16]{1,0:T(1,128)}, f32[1,16]{1,0:T(1,128)}, u32[]{:S(2)}, u32[]{:S(2)}) %collective-permute-start.8) | collective-permute-done | bytes 96 | tf_op jit(solution)/shard_map/ppermute | solution.py:37
  248.1 1.2 fusion.70
  249.3 1.3 collective-permute-start.9
  250.6 4.2 %collective-permute-done.9 = f32[1,16]{1,0:T(1,128)} collective-permute-done((f32[1,16]{1,0:T(1,128)}, f32[1,16]{1,0:T(1,128)}, u32[]{:S(2)}, u32[]{:S(2)}) %collective-permute-start.9) | collective-permute-done | bytes 96 | tf_op jit(solution)/shard_map/ppermute | solution.py:37
  254.8 1.2 fusion.66
  256.0 2.6 copy.152
  258.6 2.3 multiply_reduce_fusion.1
  260.9 1.5 copy.158
  262.4 3.9 %convolution_bitcast_fusion.3 = f32[256,256]{1,0:T(8,128)} fusion(f32[1,16,64,256]{3,2,1,0:T(8,128)S(1)} %add_add_fusion.2, f32[256,1,16,64]{0,3,2,1:T(8,128)} %bitcast.195, f32[256,16]{0,1:T(8,128)S(1)} %copy.141), kind=kOutput, calls=%fused_computation.38 | convolution fusion | flops 805568512 | bytes 2375680 | tf_op jit(solution)/shard_map/transpose(jvp())/while/body/eval_jaxpr/tgn,gkpn->tgkp/dot_general | solution.py:67
  266.3 1.6 fusion.78
  267.9 1.3 fusion.79
  269.2 1.3 collective-permute-start.12
  270.6 5.0 %fusion.12 = (f32[16,256]{1,0:T(8,128)S(1)}, f32[16,256]{1,0:T(8,128)}, f32[256,256]{1,0:T(8,128)S(1)}) fusion(f32[16,256]{1,0:T(8,128)S(1)} %copy-done.30, f32[256,256]{1,0:T(8,128)S(1)} %copy-done.24, pred[256,256]{1,0:T(8,128)(4,1)S(1)} %copy-done.33, f32[16,64,256]{2,1,0:T(8,128)S(1)} %bitcast.196, bf16[256,16,64]{0,2,1:T(8,128)(2,1)S(1)} %bitcast.213), kind=kOutput, calls=%fused_computation.12 | convolution fusion | flops 816766976 | bytes 2211840 | tf_op jit(solution)/shard_map/transpose(jvp())/while/body/eval_jaxpr/gkts,sgkp->tgkp/dot_general | solution.py:66
  275.6 8.7 %collective-permute-done.12 = bf16[1,16,64,256]{3,2,1,0:T(8,128)(2,1)S(1)} collective-permute-done((bf16[1,16,64,256]{3,2,1,0:T(8,128)(2,1)S(1)}, bf16[1,16,64,256]{3,2,1,0:T(8,128)(2,1)S(1)}, u32[]{:S(2)}, u32[]{:S(2)}) %collective-permute-start.12) | collective-permute-done | bytes 524320 | tf_op jit(solution)/shard_map/ppermute | solution.py:38
  284.4 2.0 add_convert_fusion.1
  286.4 1.5 collective-permute-start.13
  287.9 1.0 convolution_bitcast_fusion.2
  290.5 2.0 fusion.38
  292.5 21.7 %collective-permute-done.13 = bf16[1,16,64,256]{3,2,1,0:T(8,128)(2,1)S(1)} collective-permute-done((bf16[1,16,64,256]{3,2,1,0:T(8,128)(2,1)}, bf16[1,16,64,256]{3,2,1,0:T(8,128)(2,1)S(1)}, u32[]{:S(2)}, u32[]{:S(2)}) %collective-permute-start.13) | collective-permute-done | bytes 524320 | tf_op jit(solution)/shard_map/ppermute | solution.py:38
  315.1 2.5 multiply_reduce_fusion.2
  317.6 1.9 multiply_reduce_fusion.3
  319.6 4.7 %fusion.33 = f32[256,1,16,64]{0,3,2,1:T(8,128)} fusion(f32[16,64,256]{2,1,0:T(8,128)S(1)} %bitcast.197, f32[16,256]{1,0:T(8,128)S(1)} %copy-done.31, f32[256,256]{1,0:T(8,128)S(1)} %copy-done.25, pred[256,256]{1,0:T(8,128)(4,1)S(1)} %copy-done.34, f32[256,1,16,64]{0,3,2,1:T(8,128)S(1)} %get-tuple-element.429, f32[256,16]{0,1:T(8,128)S(1)} %copy-done.27), kind=kOutput, calls=%fused_computation.35 | convolution fusion | flops 810024960 | bytes 3506176 | tf_op jit(solution)/shard_map/transpose(jvp())/while/body/eval_jaxpr/gkts,sgkp->tgkp/dot_general | solution.py:66
  324.2 2.7 copy.153
  326.9 3.4 fusion.39
  330.4 1.7 copy.164
  332.8 1.2 add_add_fusion.3
  334.0 2.5 reduce-window.36
  337.3 2.2 add_convert_fusion
  (146 shorter events, 19.1 us)
Async XLA Ops:
  7.2 16.0 %copy-start = (bf16[256,256]{1,0:T(8,128)(2,1)S(1)}, bf16[256,256]{1,0:T(8,128)(2,1)}, u32[]{:S(2)}) copy-start(bf16[256,256]{1,0:T(8,128)(2,1)} %param.11) | copy-start | bytes 393220
  7.2 13.2 %copy-start.1 = (bf16[256,1024]{1,0:T(8,128)(2,1)S(1)}, bf16[256,1024]{1,0:T(8,128)(2,1)}, u32[]{:S(2)}) copy-start(bf16[256,1024]{1,0:T(8,128)(2,1)} %param.9) | copy-start | bytes 1572868
  7.2 50.0 %all-gather.3.cloned.1.call-start = ((), (), s32[]{:S(2)}) async-start(), calls=%async_computation.3 | async-start | bytes 4718592 | tf_op jit(solution)/shard_map/all_gather | solution.py:141
  10.9 7.8 %copy-start.28 = (f32[16,256]{1,0:T(8,128)}, f32[16,256]{1,0:T(8,128)S(1)}, u32[]{:S(2)}) copy-start(f32[16,256]{1,0:T(8,128)S(1)} %copy_bitcast_fusion) | copy-start | bytes 49156
  11.1 5.9 %collective-permute-start.7 = (f32[1,16]{1,0:T(1,128)S(1)}, f32[1,16]{1,0:T(1,128)S(1)}, u32[]{:S(2)}, u32[]{:S(2)}) collective-permute-start(f32[1,16]{1,0:T(1,128)S(1)} %slice_exponential_fusion), channel_id=1, source_target_pairs={{8,0},{16,8},{24,16},{32,24},{40,32},{48,40},{56,48},{64,56},{72,6... | collective-permute-start | bytes 200 | tf_op jit(solution)/shard_map/ppermute | solution.py:37
  12.4 5.8 %collective-permute-start = (f32[1,16]{1,0:T(1,128)S(1)}, f32[1,16]{1,0:T(1,128)S(1)}, u32[]{:S(2)}, u32[]{:S(2)}) collective-permute-start(f32[1,16]{1,0:T(1,128)S(1)} %slice_exponential_fusion), channel_id=1, source_target_pairs={{0,8},{8,16},{16,24},{24,32},{32,40},{40,48},{48,56},{56,64},{64,7... | collective-permute-start | bytes 200 | tf_op jit(solution)/shard_map/ppermute | solution.py:37
  19.4 0.6 copy-start.17
  19.5 4.3 %copy-start.26 = (f32[256,16]{0,1:T(8,128)}, f32[256,16]{0,1:T(8,128)S(1)}, u32[]{:S(2)}) copy-start(f32[256,16]{0,1:T(8,128)S(1)} %copy.142) | copy-start | bytes 49156
  23.2 34.1 %copy-start.2 = (f32[256,1024]{0,1:T(8,128)}, f32[256,1024]{0,1:T(8,128)S(1)}, u32[]{:S(2)}) copy-start(f32[256,1024]{0,1:T(8,128)S(1)} %copy.144) | copy-start | bytes 3145732
  23.9 13.9 %collective-permute-start.3 = (bf16[1,16,64,256]{3,2,1,0:T(8,128)(2,1)S(1)}, bf16[1,16,64,256]{3,2,1,0:T(8,128)(2,1)S(1)}, u32[]{:S(2)}, u32[]{:S(2)}) collective-permute-start(bf16[1,16,64,256]{3,2,1,0:T(8,128)(2,1)S(1)} %convert_bitcast_fusion.1), channel_id=1, source_target_pairs={{0,8},{8,16},{16,24},{24,32},{32,40},{40,48},{48,56},{56,64},{64,7... | collective-permute-start | bytes 1572872 | tf_op jit(solution)/shard_map/ppermute | solution.py:38
  28.1 37.0 %copy-start.37 = (f32[16]{0:T(128)}, f32[16]{0:T(128)S(1)}, u32[]{:S(2)}) copy-start(f32[16]{0:T(128)S(1)} %fusion.73) | copy-start | bytes 196
  38.7 16.2 %collective-permute-start.4 = (bf16[1,16,64,256]{3,2,1,0:T(8,128)(2,1)}, bf16[1,16,64,256]{3,2,1,0:T(8,128)(2,1)}, u32[]{:S(2)}, u32[]{:S(2)}) collective-permute-start(bf16[1,16,64,256]{3,2,1,0:T(8,128)(2,1)} %fusion.52), channel_id=1, source_target_pairs={{0,16},{8,24},{16,32},{24,40},{32,48},{40,56},{48,64},{56,72},{64,... | collective-permute-start | bytes 1572872 | tf_op jit(solution)/shard_map/ppermute | solution.py:38
  65.2 15.1 %copy-start.42 = (f32[16]{0:T(128)S(1)}, f32[16]{0:T(128)}, u32[]{:S(2)}) copy-start(f32[16]{0:T(128)} %param.14) | copy-start | bytes 196
  65.2 51.2 %copy-start.6 = (f32[1,16,64,256]{3,2,1,0:T(8,128)S(1)}, f32[1,16,64,256]{3,2,1,0:T(8,128)}, u32[]{:S(2)}) copy-start(f32[1,16,64,256]{3,2,1,0:T(8,128)} %multiply_add_fusion.3) | copy-start | bytes 3145732
  65.2 70.4 %all-to-all-start = ((bf16[256,4,4,512]{3,1,0,2:T(4,128)(2,1)}), bf16[256,4,4,512]{3,1,0,2:T(4,128)(2,1)}, u32[]{:S(2)}, u32[]{:S(2)}) async-start(bf16[256,4,4,512]{3,1,0,2:T(4,128)(2,1)} %copy.146), calls=%async_computation | async-start | bytes 8388608 | tf_op jit(solution)/shard_map/all_to_all | solution.py:150
  73.7 155.3 %all-gather.5.cloned.1.call-start = ((), (), s32[]{:S(2)}) async-start(), calls=%async_computation.5 | async-start | bytes 2621440 | tf_op jit(solution)/shard_map/all_gather | solution.py:191
  74.7 41.1 %collective-permute-start.1 = (f32[1,16]{1,0:T(1,128)S(1)}, f32[1,16]{1,0:T(1,128)S(1)}, u32[]{:S(2)}, u32[]{:S(2)}) collective-permute-start(f32[1,16]{1,0:T(1,128)S(1)} %get-tuple-element.416), channel_id=1, source_target_pairs={{0,16},{8,24},{16,32},{24,40},{32,48},{40,56},{48,64},{56,72},{64,... | collective-permute-start | bytes 200 | tf_op jit(solution)/shard_map/ppermute | solution.py:37
  115.8 0.6 copy-start.40
  116.4 17.4 %copy-start.41 = (f32[1,16]{1,0:T(1,128)}, f32[1,16]{1,0:T(1,128)S(1)}, u32[]{:S(2)}) copy-start(f32[1,16]{1,0:T(1,128)S(1)} %fusion.68) | copy-start | bytes 196
  116.5 25.5 %copy-start.13 = (bf16[256,256]{1,0:T(8,128)(2,1)S(1)}, bf16[256,256]{1,0:T(8,128)(2,1)}, u32[]{:S(2)}) copy-start(bf16[256,256]{1,0:T(8,128)(2,1)} %param.12) | copy-start | bytes 393220
  116.5 17.3 %collective-permute-start.5 = (bf16[1,16,64,256]{3,2,1,0:T(8,128)(2,1)S(1)}, bf16[1,16,64,256]{3,2,1,0:T(8,128)(2,1)S(1)}, u32[]{:S(2)}, u32[]{:S(2)}) collective-permute-start(bf16[1,16,64,256]{3,2,1,0:T(8,128)(2,1)S(1)} %convert_element_type.98), channel_id=1, source_target_pairs={{0,32},{8,40},{16,48},{24,56},{32,64},{40,72},{48,80},{56,88},{64,... | collective-permute-start | bytes 1572872 | tf_op jit(solution)/shard_map/ppermute | solution.py:38
  133.8 0.8 copy-start.14
  135.6 13.0 %collective-permute-start.6 = (bf16[1,16,64,256]{3,2,1,0:T(8,128)(2,1)}, bf16[1,16,64,256]{3,2,1,0:T(8,128)(2,1)}, u32[]{:S(2)}, u32[]{:S(2)}) collective-permute-start(bf16[1,16,64,256]{3,2,1,0:T(8,128)(2,1)} %multiply_add_fusion.2), channel_id=1, source_target_pairs={{0,64},{8,72},{16,80},{24,88},{32,96},{40,104},{48,112},{56,120},{... | collective-permute-start | bytes 1572872 | tf_op jit(solution)/shard_map/ppermute | solution.py:38
  143.8 4.1 %collective-permute-start.2 = (f32[1,16]{1,0:T(1,128)}, f32[1,16]{1,0:T(1,128)}, u32[]{:S(2)}, u32[]{:S(2)}) collective-permute-start(f32[1,16]{1,0:T(1,128)} %copy-done.41), channel_id=1, source_target_pairs={{0,32},{8,40},{16,48},{24,56},{32,64},{40,72},{48,80},{56,88},{64,... | collective-permute-start | bytes 200 | tf_op jit(solution)/shard_map/ppermute | solution.py:37
  147.5 3.6 %copy-start.20 = (bf16[256,1024]{0,1:T(8,128)(2,1)S(1)}, bf16[256,1024]{0,1:T(8,128)(2,1)}, u32[]{:S(2)}) copy-start(bf16[256,1024]{0,1:T(8,128)(2,1)} %copy.139) | copy-start | bytes 1572868
  147.5 3.6 %copy-start.23 = (f32[256,256]{1,0:T(8,128)S(1)}, f32[256,256]{1,0:T(8,128)}, u32[]{:S(2)}) copy-start(f32[256,256]{1,0:T(8,128)} %fusion.83) | copy-start | bytes 786436
  147.5 3.6 %copy-start.29 = (f32[16,256]{1,0:T(8,128)S(1)}, f32[16,256]{1,0:T(8,128)}, u32[]{:S(2)}) copy-start(f32[16,256]{1,0:T(8,128)} %copy-done.28) | copy-start | bytes 49156
  147.5 3.6 %copy-start.32 = (pred[256,256]{1,0:T(8,128)(4,1)S(1)}, pred[256,256]{1,0:T(8,128)(4,1)}, u32[]{:S(2)}) copy-start(pred[256,256]{1,0:T(8,128)(4,1)} %iota_compare_fusion) | copy-start | bytes 196612
  151.1 4.7 %copy-start.11 = (f32[256,1,16,64]{0,3,2,1:T(8,128)}, f32[256,1,16,64]{0,3,2,1:T(8,128)S(1)}, u32[]{:S(2)}) copy-start(f32[256,1,16,64]{0,3,2,1:T(8,128)S(1)} %convolution_bitcast_fusion.1) | copy-start | bytes 3145732
  151.2 7.2 %copy-start.16 = (bf16[256,1024]{1,0:T(8,128)(2,1)S(1)}, bf16[256,1024]{1,0:T(8,128)(2,1)}, u32[]{:S(2)}) copy-start(bf16[256,1024]{1,0:T(8,128)(2,1)} %param.10) | copy-start | bytes 1572868
  158.3 2.0 copy-start.8
  158.3 2.0 copy-start.12
  158.3 2.0 copy-start.35
  158.4 2.0 copy-start.36
  164.8 11.1 %collective-permute-start.10 = (bf16[1,16,64,256]{3,2,1,0:T(8,128)(2,1)S(1)}, bf16[1,16,64,256]{3,2,1,0:T(8,128)(2,1)S(1)}, u32[]{:S(2)}, u32[]{:S(2)}) collective-permute-start(bf16[1,16,64,256]{3,2,1,0:T(8,128)(2,1)S(1)} %convert_bitcast_fusion), channel_id=1, source_target_pairs={{8,0},{16,8},{24,16},{32,24},{40,32},{48,40},{56,48},{64,56},{72,6... | collective-permute-start | bytes 1572872 | tf_op jit(solution)/shard_map/ppermute | solution.py:38
  175.9 2.1 copy-start.9
  176.7 13.1 %collective-permute-start.11 = (bf16[1,16,64,256]{3,2,1,0:T(8,128)(2,1)S(1)}, bf16[1,16,64,256]{3,2,1,0:T(8,128)(2,1)S(1)}, u32[]{:S(2)}, u32[]{:S(2)}) collective-permute-start(bf16[1,16,64,256]{3,2,1,0:T(8,128)(2,1)S(1)} %fusion.53), channel_id=1, source_target_pairs={{16,0},{24,8},{32,16},{40,24},{48,32},{56,40},{64,48},{72,56},{80,... | collective-permute-start | bytes 1572872 | tf_op jit(solution)/shard_map/ppermute | solution.py:38
  189.9 149.6 %reduce-scatter.3.cloned.1.call-start = ((), (), s32[]{:S(2)}) async-start(), calls=%async_computation.4 | async-start | bytes 4718592 | tf_op jit(solution)/shard_map/reduce_scatter | solution.py:178
  199.7 139.8 %reduce-scatter.5.cloned.1.call-start = ((), (), s32[]{:S(2)}) async-start(), calls=%async_computation.6 | async-start | bytes 5242880 | tf_op jit(solution)/shard_map/reduce_scatter | solution.py:195
  240.9 7.1 %collective-permute-start.8 = (f32[1,16]{1,0:T(1,128)}, f32[1,16]{1,0:T(1,128)}, u32[]{:S(2)}, u32[]{:S(2)}) collective-permute-start(f32[1,16]{1,0:T(1,128)} %get-tuple-element.405), channel_id=1, source_target_pairs={{16,0},{24,8},{32,16},{40,24},{48,32},{56,40},{64,48},{72,56},{80,... | collective-permute-start | bytes 200 | tf_op jit(solution)/shard_map/ppermute | solution.py:37
  249.3 5.5 %collective-permute-start.9 = (f32[1,16]{1,0:T(1,128)}, f32[1,16]{1,0:T(1,128)}, u32[]{:S(2)}, u32[]{:S(2)}) collective-permute-start(f32[1,16]{1,0:T(1,128)} %fusion.70), channel_id=1, source_target_pairs={{32,0},{40,8},{48,16},{56,24},{64,32},{72,40},{80,48},{88,56},{96,... | collective-permute-start | bytes 200 | tf_op jit(solution)/shard_map/ppermute | solution.py:37
  262.4 8.2 %copy-start.4 = (f32[256,1024]{0,1:T(8,128)S(1)}, f32[256,1024]{0,1:T(8,128)}, u32[]{:S(2)}) copy-start(f32[256,1024]{0,1:T(8,128)} %copy.152) | copy-start | bytes 3145732
  262.4 8.2 %copy-start.21 = (bf16[256,1024]{0,1:T(8,128)(2,1)S(1)}, bf16[256,1024]{0,1:T(8,128)(2,1)}, u32[]{:S(2)}) copy-start(bf16[256,1024]{0,1:T(8,128)(2,1)} %copy.139) | copy-start | bytes 1572868
  262.4 8.2 %copy-start.24 = (f32[256,256]{1,0:T(8,128)S(1)}, f32[256,256]{1,0:T(8,128)}, u32[]{:S(2)}) copy-start(f32[256,256]{1,0:T(8,128)} %fusion.83) | copy-start | bytes 786436
  262.4 8.2 %copy-start.30 = (f32[16,256]{1,0:T(8,128)S(1)}, f32[16,256]{1,0:T(8,128)}, u32[]{:S(2)}) copy-start(f32[16,256]{1,0:T(8,128)} %copy-done.28) | copy-start | bytes 49156
  262.4 8.2 %copy-start.33 = (pred[256,256]{1,0:T(8,128)(4,1)S(1)}, pred[256,256]{1,0:T(8,128)(4,1)}, u32[]{:S(2)}) copy-start(pred[256,256]{1,0:T(8,128)(4,1)} %iota_compare_fusion) | copy-start | bytes 196612
  269.2 15.1 %collective-permute-start.12 = (bf16[1,16,64,256]{3,2,1,0:T(8,128)(2,1)S(1)}, bf16[1,16,64,256]{3,2,1,0:T(8,128)(2,1)S(1)}, u32[]{:S(2)}, u32[]{:S(2)}) collective-permute-start(bf16[1,16,64,256]{3,2,1,0:T(8,128)(2,1)S(1)} %fusion.79), channel_id=1, source_target_pairs={{32,0},{40,8},{48,16},{56,24},{64,32},{72,40},{80,48},{88,56},{96,... | collective-permute-start | bytes 1572872 | tf_op jit(solution)/shard_map/ppermute | solution.py:38
  270.6 13.8 %copy-start.10 = (bf16[1,16,64,256]{3,2,1,0:T(8,128)(2,1)S(1)}, bf16[1,16,64,256]{3,2,1,0:T(8,128)(2,1)}, u32[]{:S(2)}) copy-start(bf16[1,16,64,256]{3,2,1,0:T(8,128)(2,1)} %copy-done.9) | copy-start | bytes 1572868
  270.6 13.8 %copy-start.38 = (f32[16]{0:T(128)S(1)}, f32[16]{0:T(128)}, u32[]{:S(2)}) copy-start(f32[16]{0:T(128)} %copy-done.37) | copy-start | bytes 196
  270.6 13.8 %copy-start.39 = (f32[1,16]{1,0:T(1,128)S(1)}, f32[1,16]{1,0:T(1,128)}, u32[]{:S(2)}) copy-start(f32[1,16]{1,0:T(1,128)} %get-tuple-element.405) | copy-start | bytes 196
  275.6 13.3 %copy-start.19 = (f32[256,256]{1,0:T(8,128)}, f32[256,256]{1,0:T(8,128)S(1)}, u32[]{:S(2)}) copy-start(f32[256,256]{1,0:T(8,128)S(1)} %get-tuple-element.400) | copy-start | bytes 786436
  284.4 4.6 %copy-start.15 = (bf16[1,16,64,256]{3,2,1,0:T(8,128)(2,1)}, bf16[1,16,64,256]{3,2,1,0:T(8,128)(2,1)S(1)}, u32[]{:S(2)}) copy-start(bf16[1,16,64,256]{3,2,1,0:T(8,128)(2,1)S(1)} %collective-permute-done.12) | copy-start | bytes 1572868
  286.4 27.9 %collective-permute-start.13 = (bf16[1,16,64,256]{3,2,1,0:T(8,128)(2,1)}, bf16[1,16,64,256]{3,2,1,0:T(8,128)(2,1)S(1)}, u32[]{:S(2)}, u32[]{:S(2)}) collective-permute-start(bf16[1,16,64,256]{3,2,1,0:T(8,128)(2,1)} %add_convert_fusion.1), channel_id=1, source_target_pairs={{64,0},{72,8},{80,16},{88,24},{96,32},{104,40},{112,48},{120,56},{... | collective-permute-start | bytes 1572872 | tf_op jit(solution)/shard_map/ppermute | solution.py:38
  292.5 27.0 %copy-start.5 = (f32[256,1024]{0,1:T(8,128)S(1)}, f32[256,1024]{0,1:T(8,128)}, u32[]{:S(2)}) copy-start(f32[256,1024]{0,1:T(8,128)} %copy.152) | copy-start | bytes 3145732
  292.5 27.0 %copy-start.25 = (f32[256,256]{1,0:T(8,128)S(1)}, f32[256,256]{1,0:T(8,128)}, u32[]{:S(2)}) copy-start(f32[256,256]{1,0:T(8,128)} %fusion.83) | copy-start | bytes 786436
  292.5 27.0 %copy-start.27 = (f32[256,16]{0,1:T(8,128)S(1)}, f32[256,16]{0,1:T(8,128)}, u32[]{:S(2)}) copy-start(f32[256,16]{0,1:T(8,128)} %copy-done.26) | copy-start | bytes 49156
  292.5 27.0 %copy-start.31 = (f32[16,256]{1,0:T(8,128)S(1)}, f32[16,256]{1,0:T(8,128)}, u32[]{:S(2)}) copy-start(f32[16,256]{1,0:T(8,128)} %copy-done.28) | copy-start | bytes 49156
  292.5 27.0 %copy-start.34 = (pred[256,256]{1,0:T(8,128)(4,1)S(1)}, pred[256,256]{1,0:T(8,128)(4,1)}, u32[]{:S(2)}) copy-start(pred[256,256]{1,0:T(8,128)(4,1)} %iota_compare_fusion) | copy-start | bytes 196612
  314.3 0.8 copy-start.22
  319.5 7.4 %copy-start.3 = (f32[256,1024]{0,1:T(8,128)S(1)}, f32[256,1024]{0,1:T(8,128)}, u32[]{:S(2)}) copy-start(f32[256,1024]{0,1:T(8,128)} %copy-done.2) | copy-start | bytes 3145732
  324.2 7.9 %copy-start.18 = (f32[256,16]{1,0:T(8,128)S(1)}, f32[256,16]{1,0:T(8,128)}, u32[]{:S(2)}) copy-start(f32[256,16]{1,0:T(8,128)} %copy-done.17) | copy-start | bytes 49156
  324.2 13.1 %copy-start.7 = (f32[256,1024]{1,0:T(8,128)S(1)}, f32[256,1024]{1,0:T(8,128)}, u32[]{:S(2)}) copy-start(f32[256,1024]{1,0:T(8,128)} %get-tuple-element.408) | copy-start | bytes 3145732
Sparse Core Ops, SparseCore 0:
  10.3 34.7 all-gather.2
  190.1 38.8 all-gather.4
  232.0 38.2 reduce-scatter.2
  273.1 56.5 reduce-scatter.4
